TPU v7x, 512 devices: a whole 4x4x16 slice. The times are simulated.
512 devices in a mesh: seq: 64 (over y, z), tp: 8 (over x, core).
Axes of the slice: x: 4, y: 4, z: 16, core: 2. Of those that a mesh axis runs over, the one named last changes fastest.
Arguments:
- tokens: bfloat16 [1088, 2048], P('seq'), may hold values from -6 to 6
- norm_gain: bfloat16 [2048], replicated, may hold values from 0.099609375 to 1.8984375
- w_query: bfloat16 [2048, 2048], P(None, 'tp'), may hold values from -0.125 to 0.125
- w_key: bfloat16 [2048, 1024], P(None, 'tp'), may hold values from -0.125 to 0.125
- w_value: bfloat16 [2048, 1024], P(None, 'tp'), may hold values from -0.125 to 0.125
- w_out: bfloat16 [2048, 2048], P('tp'), may hold values from -0.125 to 0.125
- cache_keys: bfloat16 [131072, 1024], P('seq', 'tp'), may hold values from -400 to 400
- cache_values: bfloat16 [131072, 1024], P('seq', 'tp'), may hold values from -6 to 6
- cached_len: int32 [66], replicated, may hold values from 1 to 16384, 131072 in all
- block_of_shard: int32 [64], P('seq'), may hold values from 0 to 63, each once
Outputs:
- mixed: bfloat16 [1088, 2048], P('seq', 'tp')
Inputs may be any that keep to these rules, and one draw needn't show every extreme that they name: `cached_len`: they sum to exactly 131072, so every cache slot belongs to a request; the largest is 16384. `block_of_shard`: each index of seq stores a different block.
All inputs are finite; a program needn't handle non-finite values.
Results may differ from a plain program's by a relative error of at most 0.02.
Values may be sent and summed in bfloat16 or wider, within the bound.
No kernel may reach another device: no remote copies, remote signals or barrier semaphores. Data moves between devices by JAX's collectives and lax.ppermute only.
A program may use at most 192 MiB of HBM per device.

v0:
```python
import jax
import jax.numpy as jnp
from jax import lax
from jax.sharding import PartitionSpec as P

HD = 128
SPAN = 512
PREFILLS = 2


NEGATIVE = -1e30
THETA = 1000000.0
EPSILON = 1e-06


def rotate(values, places):
    half_dim = values.shape[-1] // 2
    frequency = THETA ** (-jnp.arange(half_dim, dtype=jnp.float32) / half_dim)
    angles = places.astype(jnp.float32)[:, None] * frequency[None, :]
    cosine = jnp.cos(angles)[:, None, :]
    sine_part = jnp.sin(angles)[:, None, :]
    front_half = values[..., :half_dim]
    second = values[..., half_dim:]
    return jnp.concatenate(
        [front_half * cosine - second * sine_part, second * cosine + front_half * sine_part],
        axis=-1,
    )


def row_layout(row_count, cached_len):
    position_index = jnp.arange(row_count, dtype=jnp.int32)
    boundary = PREFILLS * SPAN
    request = jnp.where(
        position_index < boundary, position_index // SPAN, PREFILLS + position_index - boundary
    )
    offset = jnp.where(position_index < boundary, position_index % SPAN, 0)
    matches = request[:, None] == jnp.arange(cached_len.shape[0], dtype=jnp.int32)[None, :]
    begins = jnp.sum(jnp.where(matches, cached_len[None, :], 0), axis=1)
    return (request, begins + offset)


def slot_layout(block_number, slot_count, cached_len):
    packed = block_number * slot_count + jnp.arange(slot_count, dtype=jnp.int32)
    ending = jnp.cumsum(cached_len)
    before = packed[:, None] >= ending[None, :]
    request = jnp.sum(before.astype(jnp.int32), axis=1)
    places = packed - jnp.sum(jnp.where(before, cached_len[None, :], 0), axis=1)
    return (request, places)


def per_device(
    tokens,
    norm_gain,
    w_query,
    w_key,
    w_value,
    w_out,
    cache_keys,
    cache_values,
    cached_len,
    block_of_shard,
):
    seq_count = lax.axis_size("seq")
    seq_index = lax.axis_index("seq")
    tok_rows = tokens.shape[0]
    all_rows = tok_rows * seq_count
    q_heads = w_query.shape[1] // HD
    kv_heads = w_key.shape[1] // HD
    head_groups = q_heads // kv_heads
    boundary = PREFILLS * SPAN
    request_all, position_all = row_layout(all_rows, cached_len)
    my_request = lax.dynamic_slice_in_dim(request_all, seq_index * tok_rows, tok_rows)
    my_position = lax.dynamic_slice_in_dim(position_all, seq_index * tok_rows, tok_rows)
    hidden = tokens.astype(jnp.float32)
    scale_row = lax.rsqrt(jnp.mean(hidden * hidden, axis=1, keepdims=True) + EPSILON)
    normed = (hidden * scale_row * norm_gain.astype(jnp.float32)[None, :]).astype(jnp.bfloat16)
    queries = jnp.dot(normed, w_query, preferred_element_type=jnp.float32).reshape(
        tok_rows, q_heads, HD
    )
    queries = rotate(queries, my_position).astype(jnp.bfloat16).reshape(tok_rows, q_heads * HD)
    new_keys = jnp.dot(normed, w_key, preferred_element_type=jnp.float32).reshape(
        tok_rows, kv_heads, HD
    )
    new_keys = rotate(new_keys, my_position).astype(jnp.bfloat16)
    new_values = (
        jnp.dot(normed, w_value, preferred_element_type=jnp.float32)
        .astype(jnp.bfloat16)
        .reshape(tok_rows, kv_heads, HD)
    )
    key_block = jnp.concatenate([cache_keys.reshape(-1, kv_heads, HD), new_keys], axis=0)
    value_block = jnp.concatenate([cache_values.reshape(-1, kv_heads, HD), new_values], axis=0)
    slot_request, slot_position = slot_layout(block_of_shard[0], cache_keys.shape[0], cached_len)
    key_request = jnp.concatenate([slot_request, my_request], axis=0)
    key_position = jnp.concatenate([slot_position, my_position], axis=0)
    gathered = lax.all_gather(queries, "seq", axis=0, tiled=True)

    def block_partial(block_item):
        q_rows, q_request, q_position = block_item
        row_count = q_rows.shape[0]
        q_four = q_rows.reshape(row_count, kv_heads, head_groups, HD)
        scores = jnp.einsum(
            "bcgd,kcd->bcgk", q_four, key_block, preferred_element_type=jnp.float32
        ) * HD ** (-0.5)
        visible = (q_request[:, None] == key_request[None, :]) & (
            key_position[None, :] <= q_position[:, None]
        )
        visible = visible[:, None, None, :]
        scores = jnp.where(visible, scores, NEGATIVE)
        row_top = jnp.max(scores, axis=-1)
        weights = jnp.where(visible, jnp.exp(scores - row_top[..., None]), 0.0)
        denominator = jnp.sum(weights, axis=-1)
        numerator = jnp.einsum(
            "bcgk,kcd->bcgd",
            weights.astype(jnp.bfloat16),
            value_block,
            preferred_element_type=jnp.float32,
        )
        return (
            row_top.reshape(row_count, q_heads),
            numerator.reshape(row_count, q_heads, HD),
            denominator.reshape(row_count, q_heads),
        )

    def prefill_block(block_item):
        return block_partial(block_item)

    prefill_parts = lax.map(
        prefill_block,
        (
            gathered[:boundary].reshape(PREFILLS, SPAN, q_heads * HD),
            request_all[:boundary].reshape(PREFILLS, SPAN),
            position_all[:boundary].reshape(PREFILLS, SPAN),
        ),
    )
    decode_parts = block_partial(
        (gathered[boundary:], request_all[boundary:], position_all[boundary:])
    )
    row_top = jnp.concatenate(
        [prefill_parts[0].reshape(boundary, q_heads), decode_parts[0]], axis=0
    )
    numerator = jnp.concatenate(
        [prefill_parts[1].reshape(boundary, q_heads, HD), decode_parts[1]], axis=0
    )
    denominator = jnp.concatenate(
        [prefill_parts[2].reshape(boundary, q_heads), decode_parts[2]], axis=0
    )
    overall = lax.pmax(row_top, "seq")
    factor = jnp.exp(row_top - overall)
    numerator, denominator = (
        lax.psum_scatter(numerator * factor[..., None], "seq", scatter_dimension=0, tiled=True),
        lax.psum_scatter(denominator * factor, "seq", scatter_dimension=0, tiled=True),
    )
    attended = (
        (numerator / denominator[..., None]).astype(jnp.bfloat16).reshape(tok_rows, q_heads * HD)
    )
    partial_out = jnp.dot(attended, w_out, preferred_element_type=jnp.float32)
    return lax.psum_scatter(partial_out.astype(jnp.bfloat16), "tp", scatter_dimension=1, tiled=True)


def solution(mesh):
    in_specs = (
        P("seq", None),
        P(),
        P(None, "tp"),
        P(None, "tp"),
        P(None, "tp"),
        P("tp", None),
        P("seq", "tp"),
        P("seq", "tp"),
        P(),
        P("seq"),
    )
    out_specs = P("seq", "tp")
    return jax.shard_map(
        per_device, mesh=mesh, in_specs=in_specs, out_specs=out_specs, check_vma=False
    )
```

profile of v0, /device:TPU:1, one launch (start us, length us, event | category | flops | bytes accessed | tf_op | source)
XLA Modules:
  0.0 604.7 jit_solution(4851465821810212221)
XLA Ops:
  6.6 0.9 select_reduce_fusion
  7.5 0.1 dynamic_slice.17
  7.6 0.7 convert_element_type.47
  8.3 1.0 fusion.33
  9.3 1.6 fusion.61
  10.9 0.1 multiply_cosine_fusion.1
  11.1 0.1 subtract_convert_fusion
  11.2 0.1 pad_maximum_fusion.2
  11.3 82.9 %all-gather = bf16[64,17,256]{2,1,0:T(8,128)(2,1)S(1)} all-gather(bf16[1,17,256]{2,1,0:T(8,128)(2,1)S(1)} %reshape.413), channel_id=1, replica_groups=mesh['seq'=64,'tp'=8] {'seq'}, dimensions={0}, use_global_device_ids=true | all-gather | bytes 565760 | tf_op jit(solution)/shard_map/all_gather | solution.py:95
  94.3 0.2 reshape.414
  94.5 0.6 copy-done.3
  95.1 0.2 copy-done.9
  95.3 0.2 convolution_bitcast_fusion.1
  95.6 0.1 fusion.48
  95.8 0.2 fusion.21
  96.0 0.1 copy.33
  96.1 0.1 reduce-window.8
  96.2 0.1 reduce.4
  97.0 0.2 fusion.24
  97.3 0.2 compare_and_fusion.1
  97.5 1.9 maximum_maximum_fusion
  99.4 0.4 fusion.64
  99.8 0.4 fusion.22
  100.2 0.4 copy-done.8
  100.6 0.4 convolution_bitcast_fusion
  101.0 0.3 slice-done.3
  101.3 0.4 slice-done
  101.7 19.6 %while.14 = (s32[]{:T(128)}, f32[2,512,2]{1,2,0:T(2,128)S(1)}, f32[2,512,2,128]{3,1,0,2:T(8,128)}, f32[2,512,2]{1,2,0:T(2,128)S(1)}, s32[2,512]{1,0:T(2,128)S(1)...) while((s32[]{:T(128)}, f32[2,512,2]{1,2,0:T(2,128)S(1)}, ...), condition=%wide.region_8.9_spmd, body=%wide.region_5.8_spmd.sunk | while | flops 1113313792 | bytes 43095140 | solution.py:127
  101.7 1.5 compare_and_fusion.3
  103.3 0.1 copy.56
  103.5 2.5 fusion.80
  106.0 3.1 fusion.82
  109.2 2.3 fusion.81
  111.5 1.5 compare_and_fusion.3
  113.1 0.1 copy.56
  113.3 2.5 fusion.80
  115.8 3.1 fusion.82
  119.0 2.3 fusion.81
  121.3 116.6 %pmax.7 = f32[1088,2]{0,1:T(2,128)S(1)} all-reduce(f32[1088,2]{0,1:T(2,128)S(1)} %pad_maximum_fusion.1), channel_id=1, replica_groups=mesh['seq'=64,'tp'=8] {'seq'}, use_global_device_ids=true, to_apply=%region_10.11 | all-reduce | flops 2176 | bytes 17408 | tf_op jit(solution)/shard_map/pmax | solution.py:147
  237.9 1.6 maximum_multiply_fusion
  239.5 4.8 copy.37
  244.4 1.3 dynamic-slice
  246.3 114.6 %all-reduce.1 = f32[1088,2]{0,1:T(2,128)S(1)} all-reduce(f32[1088,2]{0,1:T(2,128)S(1)} %get-tuple-element.135), channel_id=3, replica_groups=mesh['seq'=64,'tp'=8] {'seq'}, use_global_device_ids=true, to_apply=%region_13.14.clone | all-reduce | flops 2176 | bytes 17408
  361.0 0.1 copy.38
  361.1 191.8 %all-reduce.4.cloned.1.call-done = f32[1088,2,128]{2,1,0:T(2,128)} async-done(((f32[1088,2,128]{2,1,0:T(2,128)}), f32[1088,2,128]{2,1,0:T(2,128)}) %all-reduce.4.cloned.1.call-update) | async-done | bytes 1114128
  552.9 0.8 fusion.42
  553.8 0.9 convolution_convert_fusion
  554.7 43.2 %reduce-scatter.3.cloned.1.call-done = bf16[17,256]{1,0:T(8,128)(2,1)} async-done(((bf16[17,2048]{1,0:T(8,128)(2,1)}), bf16[17,256]{1,0:T(8,128)(2,1)}) %reduce-scatter.3.cloned.1.call-update) | async-done | bytes 8720 | tf_op jit(solution)/shard_map/reduce_scatter | solution.py:157
  (71 shorter events, 0.6 us)
Async XLA Ops:
  6.5 547.2 %copy-start = (bf16[256,2048]{1,0:T(8,128)(2,1)S(1)}, bf16[256,2048]{1,0:T(8,128)(2,1)}, u32[]{:S(2)}) copy-start(bf16[256,2048]{1,0:T(8,128)(2,1)} %param.17) | copy-start | bytes 3145732
  6.5 546.4 %all-reduce.4.cloned.1.call-start = ((), (), s32[]{:S(2)}) async-start(), calls=%async_computation.2 | async-start | bytes 2228224
  6.5 87.7 %copy-start.11 = (s32[1088]{0:T(1024)}, s32[1088]{0:T(1024)S(1)}, u32[]{:S(2)}) copy-start(s32[1088]{0:T(1024)S(1)} %fusion.52) | copy-start | bytes 13060
  7.4 86.8 %copy-start.12 = (s32[1088]{0:T(1024)}, s32[1088]{0:T(1024)S(1)}, u32[]{:S(2)}) copy-start(s32[1088]{0:T(1024)S(1)} %fusion.55) | copy-start | bytes 13060
  94.2 0.9 copy-start.3
  94.2 1.1 copy-start.9
  94.5 4.9 copy-start.1
  94.5 1.3 copy-start.10
  94.5 1.5 copy-start.13
  94.5 2.8 slice-start.2
  94.5 2.8 slice-start.4
  95.3 2.1 copy-start.7
  99.4 0.8 copy-start.2
  99.4 1.2 copy-start.8
  100.6 0.7 slice-start.3
  100.6 0.7 slice-start.1
  100.6 1.1 slice-start
  103.4 2.6 copy-start.4
  103.5 2.6 copy-start.6
  109.2 2.3 copy-start.5
  113.3 2.6 copy-start.4
  113.3 2.6 copy-start.6
  119.0 2.3 copy-start.5
  244.3 353.5 %reduce-scatter.3.cloned.1.call-start = ((), (), s32[]{:S(2)}) async-start(), calls=%async_computation.1 | async-start | bytes 110592 | tf_op jit(solution)/shard_map/reduce_scatter | solution.py:157
Sparse Core Ops, SparseCore 0:
  244.5 308.4 all-reduce.3
  555.7 42.1 reduce-scatter.2
where the time goes:
time: 606 us; the launch traced here: 605 us
  blocking collectives  314 us (52%)
  waiting for transfers between devices  235 us (39%)
  other arithmetic  16.1 us (3%)
  matrix products  15.1 us (2%)
  between operations  15 us (2%)
  local copies, waits for them, and re-layouts  9.16 us (2%)
    unnamed x3, waiting for transfers between devices  192 us
    pmax x1, blocking collectives, per_device(): overall = lax.pmax(row_top, 'seq')  117 us
    unnamed x1, blocking collectives  115 us
    all_gather x1, blocking collectives, per_device(): gathered = lax.all_gather(queries, 'seq', axis=0, tiled=True)  82.9 us
    reduce_scatter x1, waiting for transfers between devices, per_device(): lax.psum_scatter(partial_out.astype(jnp.bfloat16), 'tp', scatter_dimensio...  43.2 us
  transfers between devices with their start and end apart: 2, of which 2 were waited for; matrix products, arithmetic and copies ran while one was open for 0% of the time, Pallas kernels for 0%

commit v1 on v0

--- a/solution.py
+++ b/solution.py
@@ -1,13 +1,14 @@
 import jax
 import jax.numpy as jnp
 from jax import lax
-from jax.sharding import PartitionSpec as P
+from jax.sharding import Mesh, PartitionSpec as P
 
 HD = 128
 SPAN = 512
 PREFILLS = 2
 
 
+SEQ = ("seq_hi", "seq_lo")
 NEGATIVE = -1e30
 THETA = 1000000.0
 EPSILON = 1e-06
@@ -60,8 +61,8 @@
     cached_len,
     block_of_shard,
 ):
-    seq_count = lax.axis_size("seq")
-    seq_index = lax.axis_index("seq")
+    seq_count = lax.axis_size(SEQ)
+    seq_index = lax.axis_index(SEQ)
     tok_rows = tokens.shape[0]
     all_rows = tok_rows * seq_count
     q_heads = w_query.shape[1] // HD
@@ -92,7 +93,9 @@
     slot_request, slot_position = slot_layout(block_of_shard[0], cache_keys.shape[0], cached_len)
     key_request = jnp.concatenate([slot_request, my_request], axis=0)
     key_position = jnp.concatenate([slot_position, my_position], axis=0)
-    gathered = lax.all_gather(queries, "seq", axis=0, tiled=True)
+    gathered = lax.all_gather(
+        lax.all_gather(queries, SEQ[1], axis=0, tiled=True), SEQ[0], axis=0, tiled=True
+    )
 
     def block_partial(block_item):
         q_rows, q_request, q_position = block_item
@@ -144,12 +147,18 @@
     denominator = jnp.concatenate(
         [prefill_parts[2].reshape(boundary, q_heads), decode_parts[2]], axis=0
     )
-    overall = lax.pmax(row_top, "seq")
-    factor = jnp.exp(row_top - overall)
-    numerator, denominator = (
-        lax.psum_scatter(numerator * factor[..., None], "seq", scatter_dimension=0, tiled=True),
-        lax.psum_scatter(denominator * factor, "seq", scatter_dimension=0, tiled=True),
+    part_width = q_heads * (HD + 2)
+    packed = jnp.concatenate(
+        [numerator, denominator[..., None], row_top[..., None]], axis=-1
+    ).reshape(seq_count, tok_rows * part_width)
+    received = lax.all_to_all(packed, SEQ, 0, 0, tiled=True).reshape(
+        seq_count, tok_rows, q_heads, HD + 2
     )
+    part_top = received[..., HD + 1]
+    overall = jnp.max(part_top, axis=0)
+    factor = jnp.exp(part_top - overall[None])
+    numerator = jnp.sum(received[..., :HD] * factor[..., None], axis=0)
+    denominator = jnp.sum(received[..., HD] * factor, axis=0)
     attended = (
         (numerator / denominator[..., None]).astype(jnp.bfloat16).reshape(tok_rows, q_heads * HD)
     )
@@ -157,20 +166,34 @@
     return lax.psum_scatter(partial_out.astype(jnp.bfloat16), "tp", scatter_dimension=1, tiled=True)
 
 
+def split_mesh(mesh):
+    seq_devices = mesh.devices[:, 0]
+    try:
+        hi = len({d.coords[1] for d in seq_devices})
+    except AttributeError:
+        hi = 4
+    if seq_devices.shape[0] % hi:
+        hi = 1
+    lo = seq_devices.shape[0] // hi
+    grid = mesh.devices.reshape(hi, lo, mesh.devices.shape[1])
+    return Mesh(grid, (SEQ[0], SEQ[1], "tp"))
+
+
 def solution(mesh):
+    split = split_mesh(mesh)
     in_specs = (
-        P("seq", None),
+        P(SEQ, None),
         P(),
         P(None, "tp"),
         P(None, "tp"),
         P(None, "tp"),
         P("tp", None),
-        P("seq", "tp"),
-        P("seq", "tp"),
+        P(SEQ, "tp"),
+        P(SEQ, "tp"),
         P(),
-        P("seq"),
+        P(SEQ),
     )
-    out_specs = P("seq", "tp")
+    out_specs = P(SEQ, "tp")
     return jax.shard_map(
-        per_device, mesh=mesh, in_specs=in_specs, out_specs=out_specs, check_vma=False
+        per_device, mesh=split, in_specs=in_specs, out_specs=out_specs, check_vma=False
     )

time: 606 us -> 213 us (0.35)
  blocking collectives: 314 us -> 96.6 us
  waiting for transfers between devices: 235 us -> 41.4 us
  local copies, waits for them, and re-layouts: 9.16 us -> 22.3 us
  other arithmetic: 16.1 us -> 23.2 us
    unnamed x3 -> x1, waiting for transfers between devices: 192 us -> 0.02 us
    pmax x1 -> x0, blocking collectives: 117 us -> none  [per_device(): overall = lax.pmax(row_top, 'seq')]
    unnamed x1 -> x0, blocking collectives: 115 us -> none
    all_to_all x0 -> x1, blocking collectives: none -> 55.8 us  [per_device(): lax.all_to_all(packed, SEQ, 0, 0, tiled=True)]
    all_gather x1 -> x2, blocking collectives: 82.9 us -> 40.8 us  [the longest x1 30.2 us: per_device(): lax.all_gather(queries, SEQ[1], axis=0, tiled=True)]
  transfers between devices with their start and end apart: 2 -> 1, of which waited for: 2 -> 1; matrix products, arithmetic and copies ran while one was open for 0% -> 0% of each run, Pallas kernels for 0% -> 0%
where the time goes in v1:
time: 213 us; the launch traced here: 212 us
  blocking collectives  96.6 us (45%)
  waiting for transfers between devices  41.4 us (19%)
  other arithmetic  23.2 us (11%)
  local copies, waits for them, and re-layouts  22.3 us (10%)
  between operations  14.4 us (7%)
  matrix products  13.7 us (6%)
    all_to_all x1, blocking collectives, per_device(): lax.all_to_all(packed, SEQ, 0, 0, tiled=True)  55.8 us
    reduce_scatter x1, waiting for transfers between devices, per_device(): lax.psum_scatter(partial_out.astype(jnp.bfloat16), 'tp', scatter_dimensio...  41.4 us
    all_gather x1, blocking collectives, per_device(): lax.all_gather(queries, SEQ[1], axis=0, tiled=True)  30.2 us
    all_gather x1, blocking collectives, per_device(): lax.all_gather(lax.all_gather(queries, SEQ[1], axis=0, tiled=True), SEQ[0...  10.6 us
    dot_general x3, matrix products, block_partial(): jnp.einsum('bcgk,kcd->bcgd', weights.astype(jnp.bfloat16), value_block, p...  6.67 us
    concatenate x1, local copies, waits for them, and re-layouts, per_device(): jnp.concatenate([numerator, denominator[..., None], row_top[..., None]],...  5.64 us
    reduce_sum x3, other arithmetic, block_partial(): denominator = jnp.sum(weights, axis=-1)  4.95 us
    all_to_all x1, local copies, waits for them, and re-layouts, per_device(): lax.all_to_all(packed, SEQ, 0, 0, tiled=True)  4.34 us
  transfers between devices with their start and end apart: 1, of which 1 were waited for; matrix products, arithmetic and copies ran while one was open for 0% of the time, Pallas kernels for 0%

profile of v1, /device:TPU:1, one launch (start us, length us, event | category | flops | bytes accessed | tf_op | source)
XLA Modules:
  0.0 211.8 jit_solution(3569129755141074773)
XLA Ops:
  6.7 1.0 select_reduce_fusion
  8.4 1.0 fusion.34
  9.4 0.7 convert_element_type.51
  10.1 1.3 fusion.22
  11.5 1.3 convolution_bitcast_fusion.1
  12.8 0.1 multiply_cosine_fusion.1
  13.0 0.1 fusion.51
  13.1 0.3 fusion.64
  13.7 0.1 copy.73
  14.0 0.2 fusion.25
  14.3 30.2 %all-gather = bf16[16,17,256]{2,1,0:T(8,128)(2,1)S(1)} all-gather(bf16[1,17,256]{2,1,0:T(8,128)(2,1)S(1)} %reshape.423), channel_id=1, replica_groups=mesh['seq_hi'=4,'seq_lo'=16,'tp'=8] {'seq_lo'}, dimensions={0}, use_global_device_ids=true | all-gather | bytes 147968 | tf_op jit(solution)/shard_map/all_gather | solution.py:97
  44.5 10.6 %all_gather.7 = bf16[1088,256]{1,0:T(8,128)(2,1)S(1)} all-gather(bf16[272,256]{1,0:T(8,128)(2,1)S(1)} %reshape.424), channel_id=1, replica_groups=mesh['seq_hi'=4,'seq_lo'=16,'tp'=8] {'seq_hi'}, dimensions={0}, use_global_device_ids=true | all-gather | bytes 696320 | tf_op jit(solution)/shard_map/all_gather | solution.py:96
  55.1 0.2 compare_and_fusion.1
  55.4 0.5 copy-done.1
  55.9 0.4 fusion.68
  56.4 0.4 fusion.23
  56.8 0.4 convolution_bitcast_fusion
  57.2 0.3 slice-done.2
  57.5 0.4 slice-done
  57.8 19.1 %while.14 = (s32[]{:T(128)}, f32[2,512,2]{1,2,0:T(2,128)S(1)}, f32[2,512,2,128]{3,1,0,2:T(8,128)}, f32[2,512,2]{1,2,0:T(2,128)S(1)}, s32[2,512]{1,0:T(2,128)S(1)...) while((s32[]{:T(128)}, f32[2,512,2]{1,2,0:T(2,128)S(1)}, ...), condition=%wide.region_8.9_spmd, body=%wide.region_5.8_spmd.sunk | while | flops 1113313792 | bytes 40980560 | solution.py:130
  57.9 0.1 copy.103
  58.0 1.5 compare_and_fusion.3
  59.6 1.4 fusion.84
  61.0 2.3 %fusion.85 = f32[512,2]{0,1:T(2,128)S(1)} fusion(f32[512,2,2065]{0,2,1:T(8,128)S(1)} %get-tuple-element.249, f32[512,2]{0,1:T(2,128)S(1)} %get-tuple-element.250, pred[512,2065]{0,1:T(8,128)(4,1)S(1)} %compare_and_fusion.3), kind=kLoop, calls=%fused_computation.3.clone.1 | loop fusion | flops 10571776 | bytes 9523712 | tf_op jit(solution)/shard_map/while/body/eval_jaxpr/reduce_sum | solution.py:114
  63.3 3.1 %fusion.86 = f32[2,512,2,128]{3,1,0,2:T(8,128)S(1)} fusion(f32[2,512,2,128]{3,1,0,2:T(8,128)S(1)} %copy-done.4, s32[]{:T(128)S(6)} %copy.111, f32[512,2,2065]{0,2,1:T(8,128)S(1)} %get-tuple-element.249, f32[512,2]{0,1:T(2,128)S(1)} %get-tuple-element.250, pred[512,2065]{0,1:T(8,128)(4,1)S(1)} %compare_and_fusion.3, ...), kind=kOutput, calls=%fused_computation.10.clone.1 | convolution fusion | flops 551900160 | bytes 10606596 | tf_op jit(solution)/shard_map/while/body/eval_jaxpr/bcgk,kcd->bcgd/dot_general | solution.py:115
  66.4 1.0 copy-done.5
  67.5 0.1 copy.103
  67.6 1.5 compare_and_fusion.3
  69.2 1.4 fusion.84
  70.5 2.3 %fusion.85 = f32[512,2]{0,1:T(2,128)S(1)} fusion(f32[512,2,2065]{0,2,1:T(8,128)S(1)} %get-tuple-element.249, f32[512,2]{0,1:T(2,128)S(1)} %get-tuple-element.250, pred[512,2065]{0,1:T(8,128)(4,1)S(1)} %compare_and_fusion.3), kind=kLoop, calls=%fused_computation.3.clone.1 | loop fusion | flops 10571776 | bytes 9523712 | tf_op jit(solution)/shard_map/while/body/eval_jaxpr/reduce_sum | solution.py:114
  72.8 3.1 %fusion.86 = f32[2,512,2,128]{3,1,0,2:T(8,128)S(1)} fusion(f32[2,512,2,128]{3,1,0,2:T(8,128)S(1)} %copy-done.4, s32[]{:T(128)S(6)} %copy.111, f32[512,2,2065]{0,2,1:T(8,128)S(1)} %get-tuple-element.249, f32[512,2]{0,1:T(2,128)S(1)} %get-tuple-element.250, pred[512,2065]{0,1:T(8,128)(4,1)S(1)} %compare_and_fusion.3, ...), kind=kOutput, calls=%fused_computation.10.clone.1 | convolution fusion | flops 551900160 | bytes 10606596 | tf_op jit(solution)/shard_map/while/body/eval_jaxpr/bcgk,kcd->bcgd/dot_general | solution.py:115
  76.0 1.0 copy-done.5
  77.0 0.4 copy.77
  77.4 0.4 copy.78
  77.8 1.6 pad_maximum_fusion
  79.4 5.6 %copy.79 = f32[1088,2,130]{2,1,0:T(2,128)S(1)} copy(f32[1088,2,130]{2,0,1:T(8,128)S(1)} %pad_maximum_fusion) | data formatting | bytes 2263040 | tf_op jit(solution)/shard_map/concatenate | solution.py:151
  85.0 4.3 %all_to_all.8 = f32[64,1,4420]{2,1,0:T(1,128)} reshape(f32[1088,2,130]{2,1,0:T(2,128)S(1)} %copy.79) | data formatting | bytes 2263040 | tf_op jit(solution)/shard_map/all_to_all | solution.py:154
  89.4 55.8 %all_to_all.10 = f32[64,1,4420]{2,1,0:T(1,128)S(1)} all-to-all(f32[64,1,4420]{2,1,0:T(1,128)} %all_to_all.8), channel_id=1, replica_groups=mesh['seq_hi'=4,'seq_lo'=16,'tp'=8] {'seq_hi','seq_lo'}, dimensions={0} | all-to-all | bytes 2263040 | tf_op jit(solution)/shard_map/all_to_all | solution.py:154
  145.2 4.0 %reduce.6 = f32[64,4420]{1,0:T(8,128)} reduce(f32[64,1,4420]{2,1,0:T(1,128)S(1)} %all_to_all.10, f32[]{:T(128)} %constant.110), dimensions={1}, to_apply=%all_to_all.7.reduce_sub_computation | reduce | bytes 2263044 | tf_op jit(solution)/shard_map/all_to_all | solution.py:154
  149.2 3.3 %reshape.422 = f32[64,17,2,130]{3,2,1,0:T(2,128)S(1)} reshape(f32[64,4420]{1,0:T(8,128)} %reduce.6) | data formatting | bytes 2263040 | tf_op jit(solution)/shard_map/reshape | solution.py:154
  152.6 3.0 %fusion.67 = (f32[64,17,2,1]{3,2,1,0:T(2,128)}, f32[17,2]{1,0:T(8,128)S(1)}, f32[64,17,2,1]{3,2,1,0:T(2,128)}) fusion(f32[64,17,2,130]{3,2,1,0:T(2,128)S(1)} %reshape.422), kind=kLoop, calls=%fused_computation.108 | loop fusion | flops 2142 | bytes 34952 | tf_op jit(solution)/shard_map/slice | solution.py:161
  155.5 1.6 copy.83
  157.1 1.6 copy.88
  158.8 0.2 fusion.45
  159.0 1.2 copy.82
  160.2 2.3 %fusion.21 = f32[17,2,128]{2,1,0:T(2,128)S(1)} fusion(f32[64,17,2,130]{3,2,1,0:T(2,128)S(1)} %reshape.422, f32[64,17,2]{2,1,0:T(8,128)} %copy.82), kind=kLoop, calls=%fused_computation.29 | loop fusion | flops 552704 | bytes 1140224 | tf_op jit(solution)/shard_map/reduce_sum | solution.py:160
  162.6 0.9 convolution_convert_fusion
  163.5 41.4 %reduce-scatter.2.cloned.1.call-done = bf16[17,256]{1,0:T(8,128)(2,1)} async-done(((bf16[17,2048]{1,0:T(8,128)(2,1)}), bf16[17,256]{1,0:T(8,128)(2,1)}) %reduce-scatter.2.cloned.1.call-update) | async-done | bytes 8720 | tf_op jit(solution)/shard_map/reduce_scatter | solution.py:166
  (69 shorter events, 1.2 us)
Async XLA Ops:
  6.5 156.1 %copy-start = (bf16[256,2048]{1,0:T(8,128)(2,1)S(1)}, bf16[256,2048]{1,0:T(8,128)(2,1)}, u32[]{:S(2)}) copy-start(bf16[256,2048]{1,0:T(8,128)(2,1)} %param.17) | copy-start | bytes 3145732
  6.5 6.6 %copy-start.2 = (bf16[17,2048]{1,0:T(8,128)(2,1)S(1)}, bf16[17,2048]{1,0:T(8,128)(2,1)}, u32[]{:S(2)}) copy-start(bf16[17,2048]{1,0:T(8,128)(2,1)} %param.12) | copy-start | bytes 208900
  6.5 6.6 %copy-start.3 = (bf16[2048,256]{1,0:T(8,128)(2,1)S(1)}, bf16[2048,256]{1,0:T(8,128)(2,1)}, u32[]{:S(2)}) copy-start(bf16[2048,256]{1,0:T(8,128)(2,1)} %param.14) | copy-start | bytes 3145732
  6.5 198.4 %reduce-scatter.2.cloned.1.call-start = ((), (), s32[]{:S(2)}) async-start(), calls=%async_computation.2 | async-start | bytes 110592 | tf_op jit(solution)/shard_map/reduce_scatter | solution.py:166
  6.6 6.8 %copy-start.8 = (s32[1088]{0:T(1024)}, s32[1088]{0:T(1024)S(1)}, u32[]{:S(2)}) copy-start(s32[1088]{0:T(1024)S(1)} %fusion.55) | copy-start | bytes 13060
  7.6 5.8 %copy-start.9 = (s32[1088]{0:T(1024)}, s32[1088]{0:T(1024)S(1)}, u32[]{:S(2)}) copy-start(s32[1088]{0:T(1024)S(1)} %fusion.58) | copy-start | bytes 13060
  11.5 2.2 %copy-start.10 = (s32[66]{0:T(128)S(1)}, s32[66]{0:T(128)}, u32[]{:S(2)}) copy-start(s32[66]{0:T(128)} %param.20) | copy-start | bytes 796
  14.2 40.9 %slice-start.1 = ((s32[1088]{0:T(1024)}), s32[64]{0:T(128)S(1)}, s32[]{:S(2)}) async-start(s32[1088]{0:T(1024)} %copy-done.8), calls=%async_computation.4 | async-start | bytes 1024 | tf_op jit(solution)/shard_map/slice | solution.py:139
  14.2 40.9 %slice-start.3 = ((s32[1088]{0:T(1024)}), s32[64]{0:T(128)S(1)}, s32[]{:S(2)}) async-start(s32[1088]{0:T(1024)} %copy-done.9), calls=%async_computation.6 | async-start | bytes 1024 | tf_op jit(solution)/shard_map/slice | solution.py:139
  44.5 10.9 %copy-start.6 = (bf16[2048,128]{1,0:T(8,128)(2,1)S(1)}, bf16[2048,128]{1,0:T(8,128)(2,1)}, u32[]{:S(2)}) copy-start(bf16[2048,128]{1,0:T(8,128)(2,1)} %param.18) | copy-start | bytes 1572868
  44.5 10.9 %copy-start.7 = (bf16[2048,128]{1,0:T(8,128)(2,1)S(1)}, bf16[2048,128]{1,0:T(8,128)(2,1)}, u32[]{:S(2)}) copy-start(bf16[2048,128]{1,0:T(8,128)(2,1)} %param.19) | copy-start | bytes 1572868
  55.1 0.8 copy-start.1
  56.8 0.7 slice-start.2
  56.8 0.7 slice-start.4
  56.8 1.1 slice-start
  61.0 2.3 %copy-start.4 = (f32[2,512,2,128]{3,1,0,2:T(8,128)S(1)}, f32[2,512,2,128]{3,1,0,2:T(8,128)}, u32[]{:S(2)}) copy-start(f32[2,512,2,128]{3,1,0,2:T(8,128)} %get-tuple-element.267) | copy-start | bytes 3145732 | tf_op jit(solution)/shard_map/while
  66.4 1.0 copy-start.5
  70.5 2.3 %copy-start.4 = (f32[2,512,2,128]{3,1,0,2:T(8,128)S(1)}, f32[2,512,2,128]{3,1,0,2:T(8,128)}, u32[]{:S(2)}) copy-start(f32[2,512,2,128]{3,1,0,2:T(8,128)} %get-tuple-element.267) | copy-start | bytes 3145732 | tf_op jit(solution)/shard_map/while
  76.0 1.0 copy-start.5
Sparse Core Ops, SparseCore 0:
  163.7 41.2 reduce-scatter.1

commit v2 on v1

--- a/solution.py
+++ b/solution.py
@@ -163,7 +163,10 @@
         (numerator / denominator[..., None]).astype(jnp.bfloat16).reshape(tok_rows, q_heads * HD)
     )
     partial_out = jnp.dot(attended, w_out, preferred_element_type=jnp.float32)
-    return lax.psum_scatter(partial_out.astype(jnp.bfloat16), "tp", scatter_dimension=1, tiled=True)
+    tp_count = lax.axis_size("tp")
+    blocks = partial_out.astype(jnp.bfloat16).reshape(tok_rows, tp_count, -1).transpose(1, 0, 2)
+    blocks = lax.all_to_all(blocks, "tp", 0, 0, tiled=True)
+    return jnp.sum(blocks.astype(jnp.float32), axis=0).astype(jnp.bfloat16)
 
 
 def split_mesh(mesh):

time: 213 us -> 178 us (0.84)
  waiting for transfers between devices: 41.4 us -> 0 us
  blocking collectives: 96.6 us -> 117 us
  between operations: 14.4 us -> 1.06 us
    reduce_scatter x1 -> x0, waiting for transfers between devices: 41.4 us -> none  [per_device(): lax.psum_scatter(partial_out.astype(jnp.bfloat16), 'tp', scatter_dimensio...]
    all_to_all x0 -> x1, blocking collectives: none -> 20.5 us  [per_device(): blocks = lax.all_to_all(blocks, 'tp', 0, 0, tiled=True)]
  transfers between devices with their start and end apart: 1 -> 0, of which waited for: 1 -> 0; matrix products, arithmetic and copies ran while one was open for 0% -> 0% of each run, Pallas kernels for 0% -> 0%
where the time goes in v2:
time: 178 us
  blocking collectives  117 us (66%)
  other arithmetic  23.8 us (13%)
  local copies, waits for them, and re-layouts  22.3 us (13%)
  matrix products  13.1 us (7%)
    all_to_all x1, blocking collectives, per_device(): lax.all_to_all(packed, SEQ, 0, 0, tiled=True)  55.8 us
    all_gather x1, blocking collectives, per_device(): lax.all_gather(queries, SEQ[1], axis=0, tiled=True)  30.2 us
    all_to_all x1, blocking collectives, per_device(): blocks = lax.all_to_all(blocks, 'tp', 0, 0, tiled=True)  20.5 us
    all_gather x1, blocking collectives, per_device(): lax.all_gather(lax.all_gather(queries, SEQ[1], axis=0, tiled=True), SEQ[0...  10.6 us
    dot_general x3, matrix products, block_partial(): jnp.einsum('bcgk,kcd->bcgd', weights.astype(jnp.bfloat16), value_block, p...  6.67 us
    concatenate x1, local copies, waits for them, and re-layouts, per_device(): jnp.concatenate([numerator, denominator[..., None], row_top[..., None]],...  5.64 us
    reduce_sum x3, other arithmetic, block_partial(): denominator = jnp.sum(weights, axis=-1)  4.95 us
    all_to_all x1, local copies, waits for them, and re-layouts, per_device(): lax.all_to_all(packed, SEQ, 0, 0, tiled=True)  4.34 us

profile of v2, /device:TPU:1, one launch (start us, length us, event | category | flops | bytes accessed | tf_op | source)
XLA Modules:
  0.0 177.5 jit_solution(1448177226318435563)
XLA Ops:
  0.1 0.9 select_reduce_fusion
  1.8 1.0 fusion.34
  2.8 0.7 convert_element_type.53
  3.5 1.3 fusion.22
  4.9 1.3 convolution_bitcast_fusion.1
  6.3 0.1 multiply_cosine_fusion.1
  6.4 0.1 fusion.51
  6.5 0.3 fusion.64
  7.4 0.2 fusion.25
  7.7 30.2 %all-gather = bf16[16,17,256]{2,1,0:T(8,128)(2,1)S(1)} all-gather(bf16[1,17,256]{2,1,0:T(8,128)(2,1)S(1)} %reshape.427), channel_id=1, replica_groups=mesh['seq_hi'=4,'seq_lo'=16,'tp'=8] {'seq_lo'}, dimensions={0}, use_global_device_ids=true | all-gather | bytes 147968 | tf_op jit(solution)/shard_map/all_gather | solution.py:97
  37.9 10.6 %all_gather.7 = bf16[1088,256]{1,0:T(8,128)(2,1)S(1)} all-gather(bf16[272,256]{1,0:T(8,128)(2,1)S(1)} %reshape.428), channel_id=1, replica_groups=mesh['seq_hi'=4,'seq_lo'=16,'tp'=8] {'seq_hi'}, dimensions={0}, use_global_device_ids=true | all-gather | bytes 696320 | tf_op jit(solution)/shard_map/all_gather | solution.py:96
  48.6 0.2 compare_and_fusion.1
  48.9 0.5 copy-done.1
  49.4 0.4 fusion.68
  49.8 0.4 fusion.23
  50.2 0.4 convolution_bitcast_fusion
  50.6 0.3 slice-done.2
  50.9 0.4 slice-done
  51.3 19.1 %while.14 = (s32[]{:T(128)}, f32[2,512,2]{1,2,0:T(2,128)S(1)}, f32[2,512,2,128]{3,1,0,2:T(8,128)}, f32[2,512,2]{1,2,0:T(2,128)S(1)}, s32[2,512]{1,0:T(2,128)S(1)...) while((s32[]{:T(128)}, f32[2,512,2]{1,2,0:T(2,128)S(1)}, ...), condition=%wide.region_8.9_spmd, body=%wide.region_5.8_spmd.sunk | while | flops 1113313792 | bytes 40980560 | solution.py:130
  51.3 0.1 copy.111
  51.5 1.5 compare_and_fusion.3
  53.0 1.4 fusion.84
  54.4 2.3 %fusion.85 = f32[512,2]{0,1:T(2,128)S(1)} fusion(f32[512,2,2065]{0,2,1:T(8,128)S(1)} %get-tuple-element.249, f32[512,2]{0,1:T(2,128)S(1)} %get-tuple-element.250, pred[512,2065]{0,1:T(8,128)(4,1)S(1)} %compare_and_fusion.3), kind=kLoop, calls=%fused_computation.3.clone.1 | loop fusion | flops 10571776 | bytes 9523712 | tf_op jit(solution)/shard_map/while/body/eval_jaxpr/reduce_sum | solution.py:114
  56.7 3.1 %fusion.86 = f32[2,512,2,128]{3,1,0,2:T(8,128)S(1)} fusion(f32[2,512,2,128]{3,1,0,2:T(8,128)S(1)} %copy-done.4, s32[]{:T(128)S(6)} %copy.119, f32[512,2,2065]{0,2,1:T(8,128)S(1)} %get-tuple-element.249, f32[512,2]{0,1:T(2,128)S(1)} %get-tuple-element.250, pred[512,2065]{0,1:T(8,128)(4,1)S(1)} %compare_and_fusion.3, ...), kind=kOutput, calls=%fused_computation.10.clone.1 | convolution fusion | flops 551900160 | bytes 10606596 | tf_op jit(solution)/shard_map/while/body/eval_jaxpr/bcgk,kcd->bcgd/dot_general | solution.py:115
  59.9 1.0 copy-done.5
  60.9 0.1 copy.111
  61.0 1.5 compare_and_fusion.3
  62.6 1.4 fusion.84
  64.0 2.3 %fusion.85 = f32[512,2]{0,1:T(2,128)S(1)} fusion(f32[512,2,2065]{0,2,1:T(8,128)S(1)} %get-tuple-element.249, f32[512,2]{0,1:T(2,128)S(1)} %get-tuple-element.250, pred[512,2065]{0,1:T(8,128)(4,1)S(1)} %compare_and_fusion.3), kind=kLoop, calls=%fused_computation.3.clone.1 | loop fusion | flops 10571776 | bytes 9523712 | tf_op jit(solution)/shard_map/while/body/eval_jaxpr/reduce_sum | solution.py:114
  66.3 3.1 %fusion.86 = f32[2,512,2,128]{3,1,0,2:T(8,128)S(1)} fusion(f32[2,512,2,128]{3,1,0,2:T(8,128)S(1)} %copy-done.4, s32[]{:T(128)S(6)} %copy.119, f32[512,2,2065]{0,2,1:T(8,128)S(1)} %get-tuple-element.249, f32[512,2]{0,1:T(2,128)S(1)} %get-tuple-element.250, pred[512,2065]{0,1:T(8,128)(4,1)S(1)} %compare_and_fusion.3, ...), kind=kOutput, calls=%fused_computation.10.clone.1 | convolution fusion | flops 551900160 | bytes 10606596 | tf_op jit(solution)/shard_map/while/body/eval_jaxpr/bcgk,kcd->bcgd/dot_general | solution.py:115
  69.4 1.0 copy-done.5
  70.4 0.4 copy.81
  70.8 0.4 copy.82
  71.2 1.6 pad_maximum_fusion
  72.8 5.6 %copy.83 = f32[1088,2,130]{2,1,0:T(2,128)S(1)} copy(f32[1088,2,130]{2,0,1:T(8,128)S(1)} %pad_maximum_fusion) | data formatting | bytes 2263040 | tf_op jit(solution)/shard_map/concatenate | solution.py:151
  78.4 4.3 %all_to_all.12 = f32[64,1,4420]{2,1,0:T(1,128)} reshape(f32[1088,2,130]{2,1,0:T(2,128)S(1)} %copy.83) | data formatting | bytes 2263040 | tf_op jit(solution)/shard_map/all_to_all | solution.py:154
  82.8 55.8 %all_to_all.15 = f32[64,1,4420]{2,1,0:T(1,128)S(1)} all-to-all(f32[64,1,4420]{2,1,0:T(1,128)} %all_to_all.12), channel_id=1, replica_groups=mesh['seq_hi'=4,'seq_lo'=16,'tp'=8] {'seq_hi','seq_lo'}, dimensions={0} | all-to-all | bytes 2263040 | tf_op jit(solution)/shard_map/all_to_all | solution.py:154
  138.6 4.0 %reduce.7 = f32[64,4420]{1,0:T(8,128)} reduce(f32[64,1,4420]{2,1,0:T(1,128)S(1)} %all_to_all.15, f32[]{:T(128)} %constant.112), dimensions={1}, to_apply=%all_to_all.10.reduce_sub_computation | reduce | bytes 2263044 | tf_op jit(solution)/shard_map/all_to_all | solution.py:154
  142.6 3.3 %reshape.425 = f32[64,17,2,130]{3,2,1,0:T(2,128)S(1)} reshape(f32[64,4420]{1,0:T(8,128)} %reduce.7) | data formatting | bytes 2263040 | tf_op jit(solution)/shard_map/reshape | solution.py:154
  146.0 3.0 %fusion.67 = (f32[64,17,2,1]{3,2,1,0:T(2,128)}, f32[17,2]{1,0:T(8,128)S(1)}, f32[64,17,2,1]{3,2,1,0:T(2,128)}) fusion(f32[64,17,2,130]{3,2,1,0:T(2,128)S(1)} %reshape.425), kind=kLoop, calls=%fused_computation.109 | loop fusion | flops 2142 | bytes 34952 | tf_op jit(solution)/shard_map/slice | solution.py:161
  149.0 1.6 copy.87
  150.5 1.6 copy.93
  152.2 0.2 fusion.45
  152.4 1.2 copy.86
  153.6 2.3 %fusion.21 = f32[17,2,128]{2,1,0:T(2,128)S(1)} fusion(f32[64,17,2,130]{3,2,1,0:T(2,128)S(1)} %reshape.425, f32[64,17,2]{2,1,0:T(8,128)} %copy.86), kind=kLoop, calls=%fused_computation.29 | loop fusion | flops 552704 | bytes 1140224 | tf_op jit(solution)/shard_map/reduce_sum | solution.py:160
  156.1 0.2 convolution_convert_fusion
  156.4 20.5 %all_to_all.16 = bf16[8,17,256]{2,1,0:T(8,128)(2,1)S(1)} all-to-all(bf16[8,17,256]{2,1,0:T(8,128)(2,1)S(1)} %bitcast.165), channel_id=1, replica_groups=mesh['seq_hi'=4,'seq_lo'=16,'tp'=8] {'tp'}, dimensions={0} | all-to-all | bytes 139264 | tf_op jit(solution)/shard_map/all_to_all | solution.py:168
  176.9 0.6 reduce_sum.91
  (71 shorter events, 1.4 us)
Async XLA Ops:
  0.0 156.1 %copy-start = (bf16[256,2048]{1,0:T(8,128)(2,1)S(1)}, bf16[256,2048]{1,0:T(8,128)(2,1)}, u32[]{:S(2)}) copy-start(bf16[256,2048]{1,0:T(8,128)(2,1)} %param.17) | copy-start | bytes 3145732
  0.0 6.5 %copy-start.2 = (bf16[17,2048]{1,0:T(8,128)(2,1)S(1)}, bf16[17,2048]{1,0:T(8,128)(2,1)}, u32[]{:S(2)}) copy-start(bf16[17,2048]{1,0:T(8,128)(2,1)} %param.12) | copy-start | bytes 208900
  0.0 6.5 %copy-start.3 = (bf16[2048,256]{1,0:T(8,128)(2,1)S(1)}, bf16[2048,256]{1,0:T(8,128)(2,1)}, u32[]{:S(2)}) copy-start(bf16[2048,256]{1,0:T(8,128)(2,1)} %param.14) | copy-start | bytes 3145732
  0.0 6.8 %copy-start.8 = (s32[1088]{0:T(1024)}, s32[1088]{0:T(1024)S(1)}, u32[]{:S(2)}) copy-start(s32[1088]{0:T(1024)S(1)} %fusion.55) | copy-start | bytes 13060
  1.1 5.8 %copy-start.9 = (s32[1088]{0:T(1024)}, s32[1088]{0:T(1024)S(1)}, u32[]{:S(2)}) copy-start(s32[1088]{0:T(1024)S(1)} %fusion.58) | copy-start | bytes 13060
  4.9 2.2 %copy-start.10 = (s32[66]{0:T(128)S(1)}, s32[66]{0:T(128)}, u32[]{:S(2)}) copy-start(s32[66]{0:T(128)} %param.20) | copy-start | bytes 796
  7.7 40.9 %slice-start.1 = ((s32[1088]{0:T(1024)}), s32[64]{0:T(128)S(1)}, s32[]{:S(2)}) async-start(s32[1088]{0:T(1024)} %copy-done.8), calls=%async_computation.3 | async-start | bytes 1024 | tf_op jit(solution)/shard_map/slice | solution.py:139
  7.7 40.9 %slice-start.3 = ((s32[1088]{0:T(1024)}), s32[64]{0:T(128)S(1)}, s32[]{:S(2)}) async-start(s32[1088]{0:T(1024)} %copy-done.9), calls=%async_computation.5 | async-start | bytes 1024 | tf_op jit(solution)/shard_map/slice | solution.py:139
  37.9 10.9 %copy-start.6 = (bf16[2048,128]{1,0:T(8,128)(2,1)S(1)}, bf16[2048,128]{1,0:T(8,128)(2,1)}, u32[]{:S(2)}) copy-start(bf16[2048,128]{1,0:T(8,128)(2,1)} %param.18) | copy-start | bytes 1572868
  37.9 10.9 %copy-start.7 = (bf16[2048,128]{1,0:T(8,128)(2,1)S(1)}, bf16[2048,128]{1,0:T(8,128)(2,1)}, u32[]{:S(2)}) copy-start(bf16[2048,128]{1,0:T(8,128)(2,1)} %param.19) | copy-start | bytes 1572868
  48.5 0.8 copy-start.1
  50.2 0.7 slice-start.2
  50.2 0.7 slice-start.4
  50.2 1.1 slice-start
  54.4 2.3 %copy-start.4 = (f32[2,512,2,128]{3,1,0,2:T(8,128)S(1)}, f32[2,512,2,128]{3,1,0,2:T(8,128)}, u32[]{:S(2)}) copy-start(f32[2,512,2,128]{3,1,0,2:T(8,128)} %get-tuple-element.267) | copy-start | bytes 3145732 | tf_op jit(solution)/shard_map/while
  59.8 1.0 copy-start.5
  64.0 2.3 %copy-start.4 = (f32[2,512,2,128]{3,1,0,2:T(8,128)S(1)}, f32[2,512,2,128]{3,1,0,2:T(8,128)}, u32[]{:S(2)}) copy-start(f32[2,512,2,128]{3,1,0,2:T(8,128)} %get-tuple-element.267) | copy-start | bytes 3145732 | tf_op jit(solution)/shard_map/while
  69.4 1.0 copy-start.5

commit v3 on v2

--- a/solution.py
+++ b/solution.py
@@ -147,20 +147,30 @@
     denominator = jnp.concatenate(
         [prefill_parts[2].reshape(boundary, q_heads), decode_parts[2]], axis=0
     )
-    part_width = q_heads * (HD + 2)
+    pairs = tok_rows * q_heads
     packed = jnp.concatenate(
-        [numerator, denominator[..., None], row_top[..., None]], axis=-1
-    ).reshape(seq_count, tok_rows * part_width)
-    received = lax.all_to_all(packed, SEQ, 0, 0, tiled=True).reshape(
-        seq_count, tok_rows, q_heads, HD + 2
-    )
-    part_top = received[..., HD + 1]
-    overall = jnp.max(part_top, axis=0)
-    factor = jnp.exp(part_top - overall[None])
-    numerator = jnp.sum(received[..., :HD] * factor[..., None], axis=0)
-    denominator = jnp.sum(received[..., HD] * factor, axis=0)
+        [
+            numerator.reshape(seq_count, pairs * HD),
+            denominator.reshape(seq_count, pairs),
+            row_top.reshape(seq_count, pairs),
+        ],
+        axis=1,
+    )
+    received = lax.all_to_all(packed, SEQ, 0, 0, tiled=True)
+    part_num = received[:, : pairs * HD]
+    part_den = received[:, pairs * HD : pairs * (HD + 1)]
+    part_top = received[:, pairs * (HD + 1) :]
+    overall = jnp.max(part_top, axis=0, keepdims=True)
+    factor = jnp.exp(part_top - overall)
+    denominator = jnp.sum(part_den * factor, axis=0)
+    spread = (
+        jnp.arange(pairs, dtype=jnp.int32)[:, None]
+        == (jnp.arange(pairs * HD, dtype=jnp.int32) // HD)[None, :]
+    ).astype(jnp.float32)
+    factor_wide = jnp.dot(factor, spread, precision=lax.Precision.HIGHEST)
+    numerator = jnp.sum(part_num * factor_wide, axis=0).reshape(pairs, HD)
     attended = (
-        (numerator / denominator[..., None]).astype(jnp.bfloat16).reshape(tok_rows, q_heads * HD)
+        (numerator / denominator[:, None]).astype(jnp.bfloat16).reshape(tok_rows, q_heads * HD)
     )
     partial_out = jnp.dot(attended, w_out, preferred_element_type=jnp.float32)
     tp_count = lax.axis_size("tp")

time: 178 us -> 160 us (0.90)
  blocking collectives: 117 us -> 61.5 us
  waiting for transfers between devices: 0 us -> 46.4 us
  local copies, waits for them, and re-layouts: 22.3 us -> 10.8 us
  starting transfers between devices: 0 us -> 9.3 us
  other arithmetic: 23.8 us -> 14.6 us
  matrix products: 13.1 us -> 15.1 us
    all_to_all x1 -> x0, blocking collectives: 55.8 us -> none  [per_device(): lax.all_to_all(packed, SEQ, 0, 0, tiled=True)]
    all_to_all x0 -> x1, waiting for transfers between devices: none -> 46.4 us  [per_device(): received = lax.all_to_all(packed, SEQ, 0, 0, tiled=True)]
    all_to_all x0 -> x1, starting transfers between devices: none -> 9.3 us  [per_device(): received = lax.all_to_all(packed, SEQ, 0, 0, tiled=True)]
    all_to_all x1 -> x0, other arithmetic: 4.01 us -> none  [per_device(): lax.all_to_all(packed, SEQ, 0, 0, tiled=True)]
    slice x1 -> x0, other arithmetic: 2.98 us -> none  [per_device(): denominator = jnp.sum(received[..., HD] * factor, axis=0)]
    reduce_sum x2 -> x1, other arithmetic: 2.47 us -> 0.1 us  [per_device(): denominator = jnp.sum(part_den * factor, axis=0)]
    dot_general x3, matrix products: 3.18 us -> 5.49 us  [block_partial(): jnp.einsum('bcgd,kcd->bcgk', q_four, key_block, preferred_element_type=jn...]
    all_to_all x1, local copies, waits for them, and re-layouts: 4.34 us -> 2.18 us  [per_device(): received = lax.all_to_all(packed, SEQ, 0, 0, tiled=True)]
  transfers between devices with their start and end apart: 0 -> 1, of which waited for: 0 -> 1; matrix products, arithmetic and copies ran while one was open for 0% -> 0% of each run, Pallas kernels for 0% -> 0%
where the time goes in v3:
time: 160 us; the launch traced here: 159 us
  blocking collectives  61.5 us (38%)
  waiting for transfers between devices  46.4 us (29%)
  matrix products  15.1 us (9%)
  other arithmetic  14.6 us (9%)
  local copies, waits for them, and re-layouts  10.8 us (7%)
  starting transfers between devices  9.3 us (6%)
    all_to_all x1, waiting for transfers between devices, per_device(): received = lax.all_to_all(packed, SEQ, 0, 0, tiled=True)  46.4 us
    all_gather x1, blocking collectives, per_device(): lax.all_gather(queries, SEQ[1], axis=0, tiled=True)  30.3 us
    all_to_all x1, blocking collectives, per_device(): blocks = lax.all_to_all(blocks, 'tp', 0, 0, tiled=True)  20.6 us
    all_gather x1, blocking collectives, per_device(): lax.all_gather(lax.all_gather(queries, SEQ[1], axis=0, tiled=True), SEQ[0...  10.6 us
    all_to_all x1, starting transfers between devices, per_device(): received = lax.all_to_all(packed, SEQ, 0, 0, tiled=True)  9.3 us
    dot_general x3, matrix products, block_partial(): jnp.einsum('bcgk,kcd->bcgd', weights.astype(jnp.bfloat16), value_block, p...  6.63 us
    dot_general x3, matrix products, block_partial(): jnp.einsum('bcgd,kcd->bcgk', q_four, key_block, preferred_element_type=jn...  5.49 us
    reduce_sum x3, other arithmetic, block_partial(): denominator = jnp.sum(weights, axis=-1)  4.95 us
  transfers between devices with their start and end apart: 1, of which 1 were waited for; matrix products, arithmetic and copies ran while one was open for 0% of the time, Pallas kernels for 0%

profile of v3, /device:TPU:1, one launch (start us, length us, event | category | flops | bytes accessed | tf_op | source)
XLA Modules:
  0.0 159.0 jit_solution(16249854379726661683)
XLA Ops:
  0.0 0.9 select_reduce_fusion
  1.1 0.7 convert_element_type.51
  1.8 1.0 fusion.35
  2.8 1.6 fusion.67
  4.4 0.1 multiply_cosine_fusion.1
  4.8 30.3 %all-gather = bf16[16,17,256]{2,1,0:T(8,128)(2,1)S(1)} all-gather(bf16[1,17,256]{2,1,0:T(8,128)(2,1)S(1)} %reshape.449), channel_id=1, replica_groups=mesh['seq_hi'=4,'seq_lo'=16,'tp'=8] {'seq_lo'}, dimensions={0}, use_global_device_ids=true | all-gather | bytes 147968 | tf_op jit(solution)/shard_map/all_gather | solution.py:97
  35.2 10.6 %all_gather.7 = bf16[1088,256]{1,0:T(8,128)(2,1)S(1)} all-gather(bf16[272,256]{1,0:T(8,128)(2,1)S(1)} %reshape.450), channel_id=1, replica_groups=mesh['seq_hi'=4,'seq_lo'=16,'tp'=8] {'seq_hi'}, dimensions={0}, use_global_device_ids=true | all-gather | bytes 696320 | tf_op jit(solution)/shard_map/all_gather | solution.py:96
  45.8 0.2 convolution_bitcast_fusion.1
  46.1 0.1 fusion.54
  46.2 0.2 fusion.22
  46.5 0.1 copy.41
  46.7 0.1 reduce.5
  47.5 0.2 fusion.25
  47.8 0.2 compare_and_fusion.1
  47.9 1.9 %maximum_maximum_fusion = (bf16[2065,1,128]{2,0,1:T(8,128)(2,1)S(1)}, bf16[2065,1,128]{2,0,1:T(8,128)(2,1)}) fusion(bf16[17,1,64]{2,0,1:T(8,128)(2,1)S(1)} %get-tuple-element.144, bf16[17,1,64]{2,0,1:T(8,128)(2,1)S(1)} %get-tuple-element.143, bf16[2048,1,128]{2,0,1:T(8,128)(2,1)S(1)} %bitcast.152, bf16[17,1,128]{2,0,1:T(8,128)(2,1)S(1)} %fusion.22, ...), kind=kLoop, calls=%fused_computation.47 | loop fusion | flops 2643200 | bytes 2114560 | tf_op jit(solution)/shard_map/concatenate | solution.py:91
  49.9 0.4 fusion.70
  50.3 0.4 fusion.23
  50.7 0.4 copy-done.9
  51.1 0.4 convolution_bitcast_fusion
  51.5 0.3 slice-done.3
  51.8 0.4 slice-done
  52.2 19.6 %while.14 = (s32[]{:T(128)}, f32[2,512,2]{1,2,0:T(2,128)S(1)}, f32[2,512,2,128]{3,1,0,2:T(8,128)}, f32[2,512,2]{1,2,0:T(2,128)S(1)}, s32[2,512]{1,0:T(2,128)S(1)...) while((s32[]{:T(128)}, f32[2,512,2]{1,2,0:T(2,128)S(1)}, ...), condition=%wide.region_8.9_spmd, body=%wide.region_5.8_spmd.sunk | while | flops 1113313792 | bytes 43095140 | solution.py:130
  52.2 1.5 compare_and_fusion.3
  53.8 0.1 copy.73
  53.9 2.5 %fusion.85 = (f32[512,2]{0,1:T(2,128)S(1)}, f32[512,2,2065]{0,2,1:T(8,128)S(1)}) fusion(pred[512,2065]{0,1:T(8,128)(4,1)S(1)} %compare_and_fusion.3, bf16[512,2,128]{0,2,1:T(8,128)(2,1)S(1)} %bitcast.145, bf16[2065,1,128]{2,0,1:T(8,128)(2,1)} %get-tuple-element.261), kind=kOutput, calls=%fused_computation.2.clone.1 | convolution fusion | flops 547670016 | bytes 10310400 | tf_op jit(solution)/shard_map/while/body/eval_jaxpr/bcgd,kcd->bcgk/dot_general | solution.py:104
  56.5 3.1 %fusion.87 = f32[2,512,2,128]{3,1,0,2:T(8,128)S(1)} fusion(f32[2,512,2,128]{3,1,0,2:T(8,128)S(1)} %copy-done.4, s32[]{:T(128)} %get-tuple-element.240, f32[512,2,2065]{0,2,1:T(8,128)S(1)} %get-tuple-element.224, f32[512,2]{0,1:T(2,128)S(1)} %get-tuple-element.225, pred[512,2065]{0,1:T(8,128)(4,1)S(1)} %compare_and_fusion.3, ...), kind=kOutput, calls=%fused_computation.10.clone.1 | convolution fusion | flops 551900160 | bytes 10606596 | tf_op jit(solution)/shard_map/while/body/eval_jaxpr/bcgk,kcd->bcgd/dot_general | solution.py:115
  59.6 2.3 %fusion.86 = f32[512,2]{0,1:T(2,128)S(1)} fusion(f32[512,2,2065]{0,2,1:T(8,128)S(1)} %get-tuple-element.224, f32[512,2]{0,1:T(2,128)S(1)} %get-tuple-element.225, pred[512,2065]{0,1:T(8,128)(4,1)S(1)} %compare_and_fusion.3), kind=kLoop, calls=%fused_computation.3.clone.1 | loop fusion | flops 10571776 | bytes 9523712 | tf_op jit(solution)/shard_map/while/body/eval_jaxpr/reduce_sum | solution.py:114
  62.0 1.5 compare_and_fusion.3
  63.6 0.1 copy.73
  63.7 2.5 %fusion.85 = (f32[512,2]{0,1:T(2,128)S(1)}, f32[512,2,2065]{0,2,1:T(8,128)S(1)}) fusion(pred[512,2065]{0,1:T(8,128)(4,1)S(1)} %compare_and_fusion.3, bf16[512,2,128]{0,2,1:T(8,128)(2,1)S(1)} %bitcast.145, bf16[2065,1,128]{2,0,1:T(8,128)(2,1)} %get-tuple-element.261), kind=kOutput, calls=%fused_computation.2.clone.1 | convolution fusion | flops 547670016 | bytes 10310400 | tf_op jit(solution)/shard_map/while/body/eval_jaxpr/bcgd,kcd->bcgk/dot_general | solution.py:104
  66.3 3.1 %fusion.87 = f32[2,512,2,128]{3,1,0,2:T(8,128)S(1)} fusion(f32[2,512,2,128]{3,1,0,2:T(8,128)S(1)} %copy-done.4, s32[]{:T(128)} %get-tuple-element.240, f32[512,2,2065]{0,2,1:T(8,128)S(1)} %get-tuple-element.224, f32[512,2]{0,1:T(2,128)S(1)} %get-tuple-element.225, pred[512,2065]{0,1:T(8,128)(4,1)S(1)} %compare_and_fusion.3, ...), kind=kOutput, calls=%fused_computation.10.clone.1 | convolution fusion | flops 551900160 | bytes 10606596 | tf_op jit(solution)/shard_map/while/body/eval_jaxpr/bcgk,kcd->bcgd/dot_general | solution.py:115
  69.4 2.3 %fusion.86 = f32[512,2]{0,1:T(2,128)S(1)} fusion(f32[512,2,2065]{0,2,1:T(8,128)S(1)} %get-tuple-element.224, f32[512,2]{0,1:T(2,128)S(1)} %get-tuple-element.225, pred[512,2065]{0,1:T(8,128)(4,1)S(1)} %compare_and_fusion.3), kind=kLoop, calls=%fused_computation.3.clone.1 | loop fusion | flops 10571776 | bytes 9523712 | tf_op jit(solution)/shard_map/while/body/eval_jaxpr/reduce_sum | solution.py:114
  71.8 0.2 copy.47
  72.0 0.2 reshape.446
  72.2 0.2 copy.46
  72.5 0.2 reshape.444
  72.7 0.3 copy-done.6
  73.1 4.1 %copy.45 = f32[1088,2,128]{2,1,0:T(2,128)S(1)} copy(f32[1088,2,128]{2,0,1:T(8,128)S(1)} %pad_maximum_fusion) | data formatting | bytes 2228224 | tf_op jit(solution)/shard_map/concatenate | solution.py:144
  77.1 0.9 reshape.442
  78.0 0.3 concatenate.49
  78.3 2.2 %copy.48 = f32[64,1,4420]{2,1,0:T(1,128)} copy(f32[64,1,4420]{2,0,1:T(8,128)S(1)} %bitcast.147) | data formatting | bytes 2263040 | tf_op jit(solution)/shard_map/all_to_all | solution.py:159
  80.5 9.3 %all-to-all-start = ((f32[64,1,4420]{2,1,0:T(1,128)}), f32[64,1,4420]{2,1,0:T(1,128)S(1)}, u32[]{:S(2)}, u32[]{:S(2)}) async-start(f32[64,1,4420]{2,1,0:T(1,128)} %copy.48), calls=%async_computation | async-start | bytes 2293760 | tf_op jit(solution)/shard_map/all_to_all | solution.py:159
  89.8 46.4 %all-to-all-done = f32[64,1,4420]{2,1,0:T(1,128)S(1)} async-done(((f32[64,1,4420]{2,1,0:T(1,128)}), f32[64,1,4420]{2,1,0:T(1,128)S(1)}, u32[]{:S(2)}, u32[]{:S(2)}) %all-to-all-start) | async-done | bytes 1131552 | tf_op jit(solution)/shard_map/all_to_all | solution.py:159
  136.4 0.1 fusion.40
  136.7 0.7 fusion.21
  137.5 0.2 convolution_convert_fusion
  137.8 20.6 %all_to_all.17 = bf16[8,17,256]{2,1,0:T(8,128)(2,1)S(1)} all-to-all(bf16[8,17,256]{2,1,0:T(8,128)(2,1)S(1)} %bitcast.156), channel_id=1, replica_groups=mesh['seq_hi'=4,'seq_lo'=16,'tp'=8] {'tp'}, dimensions={0} | all-to-all | bytes 139264 | tf_op jit(solution)/shard_map/all_to_all | solution.py:178
  158.4 0.6 reduce_sum.91
  (84 shorter events, 1.3 us)
Async XLA Ops:
  0.0 137.5 %copy-start = (bf16[256,2048]{1,0:T(8,128)(2,1)S(1)}, bf16[256,2048]{1,0:T(8,128)(2,1)}, u32[]{:S(2)}) copy-start(bf16[256,2048]{1,0:T(8,128)(2,1)} %param.17) | copy-start | bytes 3145732
  0.0 45.8 %copy-start.12 = (s32[1088]{0:T(1024)}, s32[1088]{0:T(1024)S(1)}, u32[]{:S(2)}) copy-start(s32[1088]{0:T(1024)S(1)} %fusion.58) | copy-start | bytes 13060
  0.9 44.9 %copy-start.13 = (s32[1088]{0:T(1024)}, s32[1088]{0:T(1024)S(1)}, u32[]{:S(2)}) copy-start(s32[1088]{0:T(1024)S(1)} %fusion.61) | copy-start | bytes 13060
  4.8 41.0 %copy-start.3 = (bf16[17,2048]{1,0:T(8,128)(2,1)S(1)}, bf16[17,2048]{1,0:T(8,128)(2,1)}, u32[]{:S(2)}) copy-start(bf16[17,2048]{1,0:T(8,128)(2,1)} %param.12) | copy-start | bytes 208900
  4.8 41.0 %copy-start.10 = (bf16[2048,128]{1,0:T(8,128)(2,1)S(1)}, bf16[2048,128]{1,0:T(8,128)(2,1)}, u32[]{:S(2)}) copy-start(bf16[2048,128]{1,0:T(8,128)(2,1)} %param.15) | copy-start | bytes 1572868
  35.1 11.1 %copy-start.11 = (bf16[2048,128]{1,0:T(8,128)(2,1)S(1)}, bf16[2048,128]{1,0:T(8,128)(2,1)}, u32[]{:S(2)}) copy-start(bf16[2048,128]{1,0:T(8,128)(2,1)} %param.16) | copy-start | bytes 1572868
  45.8 4.1 %copy-start.1 = (bf16[1088,256]{1,0:T(8,128)(2,1)}, bf16[1088,256]{1,0:T(8,128)(2,1)S(1)}, u32[]{:S(2)}) copy-start(bf16[1088,256]{1,0:T(8,128)(2,1)S(1)} %all_gather.7) | copy-start | bytes 1671172
  45.8 0.7 copy-start.14
  45.8 1.9 %slice-start.2 = ((s32[1088]{0:T(1024)}), s32[64]{0:T(128)S(1)}, s32[]{:S(2)}) async-start(s32[1088]{0:T(1024)} %copy-done.12), calls=%async_computation.4 | async-start | bytes 1024 | tf_op jit(solution)/shard_map/slice | solution.py:139
  45.8 1.9 %slice-start.4 = ((s32[1088]{0:T(1024)}), s32[64]{0:T(128)S(1)}, s32[]{:S(2)}) async-start(s32[1088]{0:T(1024)} %copy-done.13), calls=%async_computation.6 | async-start | bytes 1024 | tf_op jit(solution)/shard_map/slice | solution.py:139
  45.8 2.1 %copy-start.8 = (bf16[2048,128]{1,0:T(8,128)(2,1)S(1)}, bf16[2048,128]{1,0:T(8,128)(2,1)}, u32[]{:S(2)}) copy-start(bf16[2048,128]{1,0:T(8,128)(2,1)} %param.18) | copy-start | bytes 1572868
  49.9 0.8 copy-start.2
  49.9 1.2 copy-start.9
  51.1 0.7 slice-start.3
  51.1 0.7 slice-start.1
  51.1 1.1 slice-start
  53.9 2.6 %copy-start.4 = (f32[2,512,2,128]{3,1,0,2:T(8,128)S(1)}, f32[2,512,2,128]{3,1,0,2:T(8,128)}, u32[]{:S(2)}) copy-start(f32[2,512,2,128]{3,1,0,2:T(8,128)} %get-tuple-element.242) | copy-start | bytes 3145732 | tf_op jit(solution)/shard_map/while
  53.9 2.6 %copy-start.7 = (bf16[2065,1,128]{2,0,1:T(8,128)(2,1)S(1)}, bf16[2065,1,128]{2,0,1:T(8,128)(2,1)}, u32[]{:S(2)}) copy-start(bf16[2065,1,128]{2,0,1:T(8,128)(2,1)} %get-tuple-element.262) | copy-start | bytes 1585924 | tf_op jit(solution)/shard_map/while
  59.6 2.3 %copy-start.5 = (f32[2,512,2,128]{3,1,0,2:T(8,128)}, f32[2,512,2,128]{3,1,0,2:T(8,128)S(1)}, u32[]{:S(2)}) copy-start(f32[2,512,2,128]{3,1,0,2:T(8,128)S(1)} %fusion.87) | copy-start | bytes 3145732 | tf_op jit(solution)/shard_map/while
  63.7 2.6 %copy-start.4 = (f32[2,512,2,128]{3,1,0,2:T(8,128)S(1)}, f32[2,512,2,128]{3,1,0,2:T(8,128)}, u32[]{:S(2)}) copy-start(f32[2,512,2,128]{3,1,0,2:T(8,128)} %get-tuple-element.242) | copy-start | bytes 3145732 | tf_op jit(solution)/shard_map/while
  63.7 2.6 %copy-start.7 = (bf16[2065,1,128]{2,0,1:T(8,128)(2,1)S(1)}, bf16[2065,1,128]{2,0,1:T(8,128)(2,1)}, u32[]{:S(2)}) copy-start(bf16[2065,1,128]{2,0,1:T(8,128)(2,1)} %get-tuple-element.262) | copy-start | bytes 1585924 | tf_op jit(solution)/shard_map/while
  69.4 2.3 %copy-start.5 = (f32[2,512,2,128]{3,1,0,2:T(8,128)}, f32[2,512,2,128]{3,1,0,2:T(8,128)S(1)}, u32[]{:S(2)}) copy-start(f32[2,512,2,128]{3,1,0,2:T(8,128)S(1)} %fusion.87) | copy-start | bytes 3145732 | tf_op jit(solution)/shard_map/while
  71.8 1.2 copy-start.6
  80.5 55.8 %all-to-all-start = ((f32[64,1,4420]{2,1,0:T(1,128)}), f32[64,1,4420]{2,1,0:T(1,128)S(1)}, u32[]{:S(2)}, u32[]{:S(2)}) async-start(f32[64,1,4420]{2,1,0:T(1,128)} %copy.48), calls=%async_computation | async-start | bytes 2293760 | tf_op jit(solution)/shard_map/all_to_all | solution.py:159

commit v4 on v3

--- a/solution.py
+++ b/solution.py
@@ -148,27 +148,35 @@
         [prefill_parts[2].reshape(boundary, q_heads), decode_parts[2]], axis=0
     )
     pairs = tok_rows * q_heads
+    seen = denominator > 0
+    average = numerator / jnp.maximum(denominator, 1.0)[..., None]
+    log_weight = jnp.where(seen, row_top + jnp.log(jnp.where(seen, denominator, 1.0)), NEGATIVE)
+    high = lax.reduce_precision(log_weight, exponent_bits=8, mantissa_bits=7)
+    rest = log_weight - high
+    middle = lax.reduce_precision(rest, exponent_bits=8, mantissa_bits=7)
+    low = rest - middle
     packed = jnp.concatenate(
         [
-            numerator.reshape(seq_count, pairs * HD),
-            denominator.reshape(seq_count, pairs),
-            row_top.reshape(seq_count, pairs),
+            average.astype(jnp.bfloat16).reshape(seq_count, pairs * HD),
+            high.astype(jnp.bfloat16).reshape(seq_count, pairs),
+            middle.astype(jnp.bfloat16).reshape(seq_count, pairs),
+            low.astype(jnp.bfloat16).reshape(seq_count, pairs),
         ],
         axis=1,
     )
     received = lax.all_to_all(packed, SEQ, 0, 0, tiled=True)
-    part_num = received[:, : pairs * HD]
-    part_den = received[:, pairs * HD : pairs * (HD + 1)]
-    part_top = received[:, pairs * (HD + 1) :]
-    overall = jnp.max(part_top, axis=0, keepdims=True)
-    factor = jnp.exp(part_top - overall)
-    denominator = jnp.sum(part_den * factor, axis=0)
+    part_avg = received[:, : pairs * HD].astype(jnp.float32)
+    tail = received[:, pairs * HD :].astype(jnp.float32).reshape(seq_count, 3, pairs)
+    part_log = tail[:, 0] + (tail[:, 1] + tail[:, 2])
+    overall = jnp.max(part_log, axis=0, keepdims=True)
+    factor = jnp.exp(part_log - overall)
+    denominator = jnp.sum(factor, axis=0)
     spread = (
         jnp.arange(pairs, dtype=jnp.int32)[:, None]
         == (jnp.arange(pairs * HD, dtype=jnp.int32) // HD)[None, :]
     ).astype(jnp.float32)
     factor_wide = jnp.dot(factor, spread, precision=lax.Precision.HIGHEST)
-    numerator = jnp.sum(part_num * factor_wide, axis=0).reshape(pairs, HD)
+    numerator = jnp.sum(part_avg * factor_wide, axis=0).reshape(pairs, HD)
     attended = (
         (numerator / denominator[:, None]).astype(jnp.bfloat16).reshape(tok_rows, q_heads * HD)
     )

time: 160 us -> 139 us (0.87)
  waiting for transfers between devices: 46.4 us -> 21.5 us
  blocking collectives: 61.5 us -> 63.5 us
    all_to_all x1, waiting for transfers between devices: 46.4 us -> 21.5 us  [per_device(): received = lax.all_to_all(packed, SEQ, 0, 0, tiled=True)]
    convert_element_type x0 -> x2, local copies, waits for them, and re-layouts: none -> 4.86 us  [per_device(): average.astype(jnp.bfloat16).reshape(seq_count, pairs * HD)]
    concatenate x2 -> x1, local copies, waits for them, and re-layouts: 4.31 us -> 0.26 us  [per_device(): jnp.concatenate([average.astype(jnp.bfloat16).reshape(seq_count, pairs *...]
    unnamed x30 -> x32, local copies, waits for them, and re-layouts: 0.99 us -> 3.37 us
    all_to_all x1, blocking collectives: 20.6 us -> 22.6 us  [per_device(): blocks = lax.all_to_all(blocks, 'tp', 0, 0, tiled=True)]
    all_to_all x1, local copies, waits for them, and re-layouts: 2.18 us -> 0.51 us  [per_device(): received = lax.all_to_all(packed, SEQ, 0, 0, tiled=True)]
where the time goes in v4:
time: 139 us; the launch traced here: 138 us
  blocking collectives  63.5 us (46%)
  waiting for transfers between devices  21.5 us (15%)
  other arithmetic  16 us (12%)
  matrix products  15.2 us (11%)
  local copies, waits for them, and re-layouts  11.5 us (8%)
  starting transfers between devices  9.3 us (7%)
    all_gather x1, blocking collectives, per_device(): lax.all_gather(queries, SEQ[1], axis=0, tiled=True)  30.3 us
    all_to_all x1, blocking collectives, per_device(): blocks = lax.all_to_all(blocks, 'tp', 0, 0, tiled=True)  22.6 us
    all_to_all x1, waiting for transfers between devices, per_device(): received = lax.all_to_all(packed, SEQ, 0, 0, tiled=True)  21.5 us
    all_gather x1, blocking collectives, per_device(): lax.all_gather(lax.all_gather(queries, SEQ[1], axis=0, tiled=True), SEQ[0...  10.6 us
    all_to_all x1, starting transfers between devices, per_device(): received = lax.all_to_all(packed, SEQ, 0, 0, tiled=True)  9.3 us
    dot_general x3, matrix products, block_partial(): jnp.einsum('bcgk,kcd->bcgd', weights.astype(jnp.bfloat16), value_block, p...  6.63 us
    dot_general x3, matrix products, block_partial(): jnp.einsum('bcgd,kcd->bcgk', q_four, key_block, preferred_element_type=jn...  5.49 us
    reduce_sum x3, other arithmetic, block_partial(): denominator = jnp.sum(weights, axis=-1)  4.95 us
  transfers between devices with their start and end apart: 1, of which 1 were waited for; matrix products, arithmetic and copies ran while one was open for 0% of the time, Pallas kernels for 0%

profile of v4, /device:TPU:1, one launch (start us, length us, event | category | flops | bytes accessed | tf_op | source)
XLA Modules:
  0.0 138.3 jit_solution(10090682002029243600)
XLA Ops:
  0.0 0.9 select_reduce_fusion
  1.1 0.7 convert_element_type.74
  1.8 1.0 fusion.36
  2.8 1.6 %fusion.74 = f32[17,256]{1,0:T(8,128)S(1)} fusion(bf16[2048,256]{1,0:T(8,128)(2,1)} %param.14, bf16[17,2048]{1,0:T(8,128)(2,1)} %param.12, f32[2048]{0:T(1024)S(1)} %convert_element_type.74, f32[17]{0:T(128)S(1)} %add_rsqrt_fusion), kind=kOutput, calls=%fused_computation.129 | convolution fusion | flops 17965056 | bytes 1143876 | tf_op jit(solution)/shard_map/dot_general | solution.py:78
  4.8 30.3 %all-gather = bf16[16,17,256]{2,1,0:T(8,128)(2,1)S(1)} all-gather(bf16[1,17,256]{2,1,0:T(8,128)(2,1)S(1)} %reshape.477), channel_id=1, replica_groups=mesh['seq_hi'=4,'seq_lo'=16,'tp'=8] {'seq_lo'}, dimensions={0}, use_global_device_ids=true | all-gather | bytes 147968 | tf_op jit(solution)/shard_map/all_gather | solution.py:97
  35.2 10.6 %all_gather.7 = bf16[1088,256]{1,0:T(8,128)(2,1)S(1)} all-gather(bf16[272,256]{1,0:T(8,128)(2,1)S(1)} %reshape.478), channel_id=1, replica_groups=mesh['seq_hi'=4,'seq_lo'=16,'tp'=8] {'seq_hi'}, dimensions={0}, use_global_device_ids=true | all-gather | bytes 696320 | tf_op jit(solution)/shard_map/all_gather | solution.py:96
  45.8 0.2 convolution_bitcast_fusion.1
  46.2 0.2 fusion.23
  47.5 0.2 fusion.26
  47.8 0.2 compare_and_fusion.1
  47.9 1.9 %maximum_maximum_fusion = (bf16[2065,1,128]{2,0,1:T(8,128)(2,1)S(1)}, bf16[2065,1,128]{2,0,1:T(8,128)(2,1)}) fusion(bf16[17,1,64]{2,0,1:T(8,128)(2,1)S(1)} %get-tuple-element.149, bf16[17,1,64]{2,0,1:T(8,128)(2,1)S(1)} %get-tuple-element.148, bf16[2048,1,128]{2,0,1:T(8,128)(2,1)S(1)} %bitcast.160, bf16[17,1,128]{2,0,1:T(8,128)(2,1)S(1)} %fusion.23, ...), kind=kLoop, calls=%fused_computation.48 | loop fusion | flops 2643200 | bytes 2114560 | tf_op jit(solution)/shard_map/concatenate | solution.py:91
  49.9 0.4 fusion.79
  50.3 0.4 fusion.24
  50.7 0.4 copy-done.9
  51.1 0.4 convolution_bitcast_fusion
  51.5 0.3 slice-done.3
  51.8 0.4 slice-done
  52.2 19.6 %while.14 = (s32[]{:T(128)}, f32[2,512,2]{1,2,0:T(2,128)S(1)}, f32[2,512,2,128]{3,1,0,2:T(8,128)}, f32[2,512,2]{1,2,0:T(2,128)S(1)}, s32[2,512]{1,0:T(2,128)S(1)...) while((s32[]{:T(128)}, f32[2,512,2]{1,2,0:T(2,128)S(1)}, ...), condition=%wide.region_8.9_spmd, body=%wide.region_5.8_spmd.sunk | while | flops 1113313792 | bytes 43095140 | solution.py:130
  52.2 1.5 %compare_and_fusion.3 = pred[512,2065]{0,1:T(8,128)(4,1)S(1)} fusion(s32[512]{0:T(512)S(1)} %bitcast.166, s32[512]{0:T(512)S(1)} %bitcast.167, s32[2065]{0:T(1024)S(1)} %get-tuple-element.265, s32[2065]{0:T(1024)S(1)} %get-tuple-element.264), kind=kLoop, calls=%fused_computation.8.clone.1 | loop fusion | flops 3171840 | bytes 1077896 | tf_op jit(solution)/shard_map/while/body/eval_jaxpr/and | solution.py:107
  53.8 0.1 copy.78
  53.9 2.5 %fusion.94 = (f32[512,2]{0,1:T(2,128)S(1)}, f32[512,2,2065]{0,2,1:T(8,128)S(1)}) fusion(pred[512,2065]{0,1:T(8,128)(4,1)S(1)} %compare_and_fusion.3, bf16[512,2,128]{0,2,1:T(8,128)(2,1)S(1)} %bitcast.154, bf16[2065,1,128]{2,0,1:T(8,128)(2,1)} %get-tuple-element.268), kind=kOutput, calls=%fused_computation.2.clone.1 | convolution fusion | flops 547670016 | bytes 10310400 | tf_op jit(solution)/shard_map/while/body/eval_jaxpr/bcgd,kcd->bcgk/dot_general | solution.py:104
  56.5 3.1 %fusion.96 = f32[2,512,2,128]{3,1,0,2:T(8,128)S(1)} fusion(f32[2,512,2,128]{3,1,0,2:T(8,128)S(1)} %copy-done.4, s32[]{:T(128)} %get-tuple-element.247, f32[512,2,2065]{0,2,1:T(8,128)S(1)} %get-tuple-element.231, f32[512,2]{0,1:T(2,128)S(1)} %get-tuple-element.232, pred[512,2065]{0,1:T(8,128)(4,1)S(1)} %compare_and_fusion.3, ...), kind=kOutput, calls=%fused_computation.10.clone.1 | convolution fusion | flops 551900160 | bytes 10606596 | tf_op jit(solution)/shard_map/while/body/eval_jaxpr/bcgk,kcd->bcgd/dot_general | solution.py:115
  59.6 2.3 %fusion.95 = f32[512,2]{0,1:T(2,128)S(1)} fusion(f32[512,2,2065]{0,2,1:T(8,128)S(1)} %get-tuple-element.231, f32[512,2]{0,1:T(2,128)S(1)} %get-tuple-element.232, pred[512,2065]{0,1:T(8,128)(4,1)S(1)} %compare_and_fusion.3), kind=kLoop, calls=%fused_computation.3.clone.1 | loop fusion | flops 10571776 | bytes 9523712 | tf_op jit(solution)/shard_map/while/body/eval_jaxpr/reduce_sum | solution.py:114
  62.0 1.5 %compare_and_fusion.3 = pred[512,2065]{0,1:T(8,128)(4,1)S(1)} fusion(s32[512]{0:T(512)S(1)} %bitcast.166, s32[512]{0:T(512)S(1)} %bitcast.167, s32[2065]{0:T(1024)S(1)} %get-tuple-element.265, s32[2065]{0:T(1024)S(1)} %get-tuple-element.264), kind=kLoop, calls=%fused_computation.8.clone.1 | loop fusion | flops 3171840 | bytes 1077896 | tf_op jit(solution)/shard_map/while/body/eval_jaxpr/and | solution.py:107
  63.6 0.1 copy.78
  63.7 2.5 %fusion.94 = (f32[512,2]{0,1:T(2,128)S(1)}, f32[512,2,2065]{0,2,1:T(8,128)S(1)}) fusion(pred[512,2065]{0,1:T(8,128)(4,1)S(1)} %compare_and_fusion.3, bf16[512,2,128]{0,2,1:T(8,128)(2,1)S(1)} %bitcast.154, bf16[2065,1,128]{2,0,1:T(8,128)(2,1)} %get-tuple-element.268), kind=kOutput, calls=%fused_computation.2.clone.1 | convolution fusion | flops 547670016 | bytes 10310400 | tf_op jit(solution)/shard_map/while/body/eval_jaxpr/bcgd,kcd->bcgk/dot_general | solution.py:104
  66.3 3.1 %fusion.96 = f32[2,512,2,128]{3,1,0,2:T(8,128)S(1)} fusion(f32[2,512,2,128]{3,1,0,2:T(8,128)S(1)} %copy-done.4, s32[]{:T(128)} %get-tuple-element.247, f32[512,2,2065]{0,2,1:T(8,128)S(1)} %get-tuple-element.231, f32[512,2]{0,1:T(2,128)S(1)} %get-tuple-element.232, pred[512,2065]{0,1:T(8,128)(4,1)S(1)} %compare_and_fusion.3, ...), kind=kOutput, calls=%fused_computation.10.clone.1 | convolution fusion | flops 551900160 | bytes 10606596 | tf_op jit(solution)/shard_map/while/body/eval_jaxpr/bcgk,kcd->bcgd/dot_general | solution.py:115
  69.4 2.3 %fusion.95 = f32[512,2]{0,1:T(2,128)S(1)} fusion(f32[512,2,2065]{0,2,1:T(8,128)S(1)} %get-tuple-element.231, f32[512,2]{0,1:T(2,128)S(1)} %get-tuple-element.232, pred[512,2065]{0,1:T(8,128)(4,1)S(1)} %compare_and_fusion.3), kind=kLoop, calls=%fused_computation.3.clone.1 | loop fusion | flops 10571776 | bytes 9523712 | tf_op jit(solution)/shard_map/while/body/eval_jaxpr/reduce_sum | solution.py:114
  71.8 0.2 copy.50
  72.0 0.2 concatenate.61
  72.3 0.2 copy.49
  72.5 0.2 concatenate.59
  72.7 0.3 copy-done.6
  73.0 0.4 fusion.22
  73.4 4.6 %copy.48 = bf16[1088,2,128]{2,1,0:T(2,128)(2,1)S(1)} copy(bf16[1088,2,128]{2,0,1:T(8,128)(2,1)S(1)} %fusion.22) | data formatting | bytes 1114112 | tf_op jit(solution)/shard_map/convert_element_type | solution.py:160
  78.0 0.2 convert_element_type.81
  78.3 0.3 concatenate.62
  78.5 0.5 broadcast.295
  79.1 1.0 reduce.7
  80.0 1.5 %reshape.486 = bf16[64,2,2227]{2,1,0:T(2,128)(2,1)} reshape(bf16[64,4454]{1,0:T(8,128)(2,1)S(1)} %reduce.7) | data formatting | bytes 1140224
  81.5 9.3 %all-to-all-start = ((bf16[64,2,2227]{2,1,0:T(2,128)(2,1)}), bf16[64,2,2227]{2,1,0:T(2,128)(2,1)S(1)}, u32[]{:S(2)}, u32[]{:S(2)}) async-start(bf16[64,2,2227]{2,1,0:T(2,128)(2,1)} %reshape.486), calls=%async_computation | async-start | bytes 1179648 | tf_op jit(solution)/shard_map/all_to_all | solution.py:167
  90.8 21.5 %all-to-all-done = bf16[64,2,2227]{2,1,0:T(2,128)(2,1)S(1)} async-done(((bf16[64,2,2227]{2,1,0:T(2,128)(2,1)}), bf16[64,2,2227]{2,1,0:T(2,128)(2,1)S(1)}, u32[]{:S(2)}, u32[]{:S(2)}) %all-to-all-start) | async-done | bytes 570144 | tf_op jit(solution)/shard_map/all_to_all | solution.py:167
  112.3 0.9 reshape.487
  113.5 0.2 fusion.53
  114.0 0.8 fusion.21
  114.8 0.2 convolution_convert_fusion
  115.1 22.6 %all_to_all.17 = bf16[8,17,256]{2,1,0:T(8,128)(2,1)S(1)} all-to-all(bf16[8,17,256]{2,1,0:T(8,128)(2,1)S(1)} %bitcast.164), channel_id=1, replica_groups=mesh['seq_hi'=4,'seq_lo'=16,'tp'=8] {'tp'}, dimensions={0} | all-to-all | bytes 139264 | tf_op jit(solution)/shard_map/all_to_all | solution.py:186
  137.7 0.6 reduce_sum.91
  (91 shorter events, 1.9 us)
Async XLA Ops:
  0.0 114.7 %copy-start = (bf16[256,2048]{1,0:T(8,128)(2,1)S(1)}, bf16[256,2048]{1,0:T(8,128)(2,1)}, u32[]{:S(2)}) copy-start(bf16[256,2048]{1,0:T(8,128)(2,1)} %param.17) | copy-start | bytes 3145732
  0.0 45.8 %copy-start.12 = (s32[1088]{0:T(1024)}, s32[1088]{0:T(1024)S(1)}, u32[]{:S(2)}) copy-start(s32[1088]{0:T(1024)S(1)} %fusion.64) | copy-start | bytes 13060
  0.9 44.9 %copy-start.13 = (s32[1088]{0:T(1024)}, s32[1088]{0:T(1024)S(1)}, u32[]{:S(2)}) copy-start(s32[1088]{0:T(1024)S(1)} %fusion.68) | copy-start | bytes 13060
  4.8 41.0 %copy-start.3 = (bf16[17,2048]{1,0:T(8,128)(2,1)S(1)}, bf16[17,2048]{1,0:T(8,128)(2,1)}, u32[]{:S(2)}) copy-start(bf16[17,2048]{1,0:T(8,128)(2,1)} %param.12) | copy-start | bytes 208900
  4.8 41.0 %copy-start.10 = (bf16[2048,128]{1,0:T(8,128)(2,1)S(1)}, bf16[2048,128]{1,0:T(8,128)(2,1)}, u32[]{:S(2)}) copy-start(bf16[2048,128]{1,0:T(8,128)(2,1)} %param.15) | copy-start | bytes 1572868
  35.1 11.1 %copy-start.11 = (bf16[2048,128]{1,0:T(8,128)(2,1)S(1)}, bf16[2048,128]{1,0:T(8,128)(2,1)}, u32[]{:S(2)}) copy-start(bf16[2048,128]{1,0:T(8,128)(2,1)} %param.16) | copy-start | bytes 1572868
  45.8 4.1 %copy-start.1 = (bf16[1088,256]{1,0:T(8,128)(2,1)}, bf16[1088,256]{1,0:T(8,128)(2,1)S(1)}, u32[]{:S(2)}) copy-start(bf16[1088,256]{1,0:T(8,128)(2,1)S(1)} %all_gather.7) | copy-start | bytes 1671172
  45.8 0.7 copy-start.14
  45.8 1.9 %slice-start.2 = ((s32[1088]{0:T(1024)}), s32[64]{0:T(128)S(1)}, s32[]{:S(2)}) async-start(s32[1088]{0:T(1024)} %copy-done.12), calls=%async_computation.4 | async-start | bytes 1024 | tf_op jit(solution)/shard_map/slice | solution.py:139
  45.8 1.9 %slice-start.4 = ((s32[1088]{0:T(1024)}), s32[64]{0:T(128)S(1)}, s32[]{:S(2)}) async-start(s32[1088]{0:T(1024)} %copy-done.13), calls=%async_computation.6 | async-start | bytes 1024 | tf_op jit(solution)/shard_map/slice | solution.py:139
  45.8 2.1 %copy-start.8 = (bf16[2048,128]{1,0:T(8,128)(2,1)S(1)}, bf16[2048,128]{1,0:T(8,128)(2,1)}, u32[]{:S(2)}) copy-start(bf16[2048,128]{1,0:T(8,128)(2,1)} %param.18) | copy-start | bytes 1572868
  49.9 0.8 copy-start.2
  49.9 1.2 copy-start.9
  51.1 0.7 slice-start.3
  51.1 0.7 slice-start.1
  51.1 1.1 slice-start
  53.9 2.6 %copy-start.4 = (f32[2,512,2,128]{3,1,0,2:T(8,128)S(1)}, f32[2,512,2,128]{3,1,0,2:T(8,128)}, u32[]{:S(2)}) copy-start(f32[2,512,2,128]{3,1,0,2:T(8,128)} %get-tuple-element.249) | copy-start | bytes 3145732 | tf_op jit(solution)/shard_map/while
  53.9 2.6 %copy-start.7 = (bf16[2065,1,128]{2,0,1:T(8,128)(2,1)S(1)}, bf16[2065,1,128]{2,0,1:T(8,128)(2,1)}, u32[]{:S(2)}) copy-start(bf16[2065,1,128]{2,0,1:T(8,128)(2,1)} %get-tuple-element.269) | copy-start | bytes 1585924 | tf_op jit(solution)/shard_map/while
  59.6 2.3 %copy-start.5 = (f32[2,512,2,128]{3,1,0,2:T(8,128)}, f32[2,512,2,128]{3,1,0,2:T(8,128)S(1)}, u32[]{:S(2)}) copy-start(f32[2,512,2,128]{3,1,0,2:T(8,128)S(1)} %fusion.96) | copy-start | bytes 3145732 | tf_op jit(solution)/shard_map/while
  63.7 2.6 %copy-start.4 = (f32[2,512,2,128]{3,1,0,2:T(8,128)S(1)}, f32[2,512,2,128]{3,1,0,2:T(8,128)}, u32[]{:S(2)}) copy-start(f32[2,512,2,128]{3,1,0,2:T(8,128)} %get-tuple-element.249) | copy-start | bytes 3145732 | tf_op jit(solution)/shard_map/while
  63.7 2.6 %copy-start.7 = (bf16[2065,1,128]{2,0,1:T(8,128)(2,1)S(1)}, bf16[2065,1,128]{2,0,1:T(8,128)(2,1)}, u32[]{:S(2)}) copy-start(bf16[2065,1,128]{2,0,1:T(8,128)(2,1)} %get-tuple-element.269) | copy-start | bytes 1585924 | tf_op jit(solution)/shard_map/while
  69.4 2.3 %copy-start.5 = (f32[2,512,2,128]{3,1,0,2:T(8,128)}, f32[2,512,2,128]{3,1,0,2:T(8,128)S(1)}, u32[]{:S(2)}) copy-start(f32[2,512,2,128]{3,1,0,2:T(8,128)S(1)} %fusion.96) | copy-start | bytes 3145732 | tf_op jit(solution)/shard_map/while
  71.8 1.2 copy-start.6
  81.5 30.8 %all-to-all-start = ((bf16[64,2,2227]{2,1,0:T(2,128)(2,1)}), bf16[64,2,2227]{2,1,0:T(2,128)(2,1)S(1)}, u32[]{:S(2)}, u32[]{:S(2)}) async-start(bf16[64,2,2227]{2,1,0:T(2,128)(2,1)} %reshape.486), calls=%async_computation | async-start | bytes 1179648 | tf_op jit(solution)/shard_map/all_to_all | solution.py:167

commit v5 on v4

--- a/solution.py
+++ b/solution.py
@@ -1,6 +1,9 @@
+import functools
+
 import jax
 import jax.numpy as jnp
 from jax import lax
+from jax.experimental import pallas as pl
 from jax.sharding import Mesh, PartitionSpec as P
 
 HD = 128
@@ -47,6 +50,80 @@
     request = jnp.sum(before.astype(jnp.int32), axis=1)
     places = packed - jnp.sum(jnp.where(before, cached_len[None, :], 0), axis=1)
     return (request, places)
+
+
+def attend_kernel(
+    q_ref, qr_ref, qp_ref, k_ref, v_ref, kr_ref, kp_ref, nk_ref, nv_ref, nr_ref, np_ref,
+    avg_ref, lw_ref, *, heads
+):
+    seen_cache = (qr_ref[...] == kr_ref[...]) & (kp_ref[...] <= qp_ref[...])
+    seen_new = (qr_ref[...] == nr_ref[...]) & (np_ref[...] <= qp_ref[...])
+    tops = []
+    for g in range(heads):
+        qg = q_ref[:, g * HD:(g + 1) * HD]
+        dims = (((1,), (1,)), ((), ()))
+        cache_scores = lax.dot_general(
+            qg, k_ref[...], dims, preferred_element_type=jnp.float32
+        ) * HD ** (-0.5)
+        new_scores = lax.dot_general(
+            qg, nk_ref[...], dims, preferred_element_type=jnp.float32
+        ) * HD ** (-0.5)
+        cache_scores = jnp.where(seen_cache, cache_scores, NEGATIVE)
+        new_scores = jnp.where(seen_new, new_scores, NEGATIVE)
+        top = jnp.maximum(
+            jnp.max(cache_scores, axis=1, keepdims=True), jnp.max(new_scores, axis=1, keepdims=True)
+        )
+        cache_weights = jnp.exp(cache_scores - top)
+        new_weights = jnp.exp(new_scores - top)
+        den = jnp.sum(cache_weights, axis=1, keepdims=True) + jnp.sum(
+            new_weights, axis=1, keepdims=True
+        )
+        num = jnp.dot(
+            cache_weights.astype(jnp.bfloat16), v_ref[...], preferred_element_type=jnp.float32
+        ) + jnp.dot(new_weights.astype(jnp.bfloat16), nv_ref[...], preferred_element_type=jnp.float32)
+        some = top > 0.5 * NEGATIVE
+        avg_ref[:, g * HD:(g + 1) * HD] = jnp.where(some, num / den, 0.0).astype(avg_ref.dtype)
+        tops.append(jnp.where(some, top + jnp.log(den), NEGATIVE))
+    lw_ref[...] = jnp.concatenate(tops, axis=1)
+
+
+def attend(q, q_req, q_pos, keys, values, k_req, k_pos, new_k, new_v, n_req, n_pos, block_rows=136):
+    rows, width = q.shape
+    heads = width // HD
+    slots = keys.shape[0]
+    fresh = new_k.shape[0]
+    grid = (rows // block_rows,)
+    row_block = lambda i: (i, 0)
+    whole = lambda i: (0, 0)
+    return pl.pallas_call(
+        functools.partial(attend_kernel, heads=heads),
+        grid=grid,
+        in_specs=[
+            pl.BlockSpec((block_rows, width), row_block),
+            pl.BlockSpec((block_rows, 1), row_block),
+            pl.BlockSpec((block_rows, 1), row_block),
+            pl.BlockSpec((slots, HD), whole),
+            pl.BlockSpec((slots, HD), whole),
+            pl.BlockSpec((1, slots), whole),
+            pl.BlockSpec((1, slots), whole),
+            pl.BlockSpec((fresh, HD), whole),
+            pl.BlockSpec((fresh, HD), whole),
+            pl.BlockSpec((1, fresh), whole),
+            pl.BlockSpec((1, fresh), whole),
+        ],
+        out_specs=[
+            pl.BlockSpec((block_rows, width), row_block),
+            pl.BlockSpec((block_rows, heads), row_block),
+        ],
+        out_shape=[
+            jax.ShapeDtypeStruct((rows, width), jnp.bfloat16),
+            jax.ShapeDtypeStruct((rows, heads), jnp.float32),
+        ],
+    )(
+        q, q_req.reshape(rows, 1), q_pos.reshape(rows, 1), keys, values,
+        k_req.reshape(1, slots), k_pos.reshape(1, slots),
+        new_k, new_v, n_req.reshape(1, fresh), n_pos.reshape(1, fresh),
+    )
 
 
 def per_device(
@@ -88,69 +165,24 @@
         .astype(jnp.bfloat16)
         .reshape(tok_rows, kv_heads, HD)
     )
-    key_block = jnp.concatenate([cache_keys.reshape(-1, kv_heads, HD), new_keys], axis=0)
-    value_block = jnp.concatenate([cache_values.reshape(-1, kv_heads, HD), new_values], axis=0)
+    extra = -(-tok_rows // 128) * 128 - tok_rows
+    new_k = jnp.concatenate(
+        [new_keys.reshape(tok_rows, HD), jnp.zeros((extra, HD), jnp.bfloat16)], axis=0
+    )
+    new_v = jnp.concatenate(
+        [new_values.reshape(tok_rows, HD), jnp.zeros((extra, HD), jnp.bfloat16)], axis=0
+    )
+    new_req = jnp.concatenate([my_request, jnp.full((extra,), -1, jnp.int32)], axis=0)
+    new_pos = jnp.concatenate([my_position, jnp.zeros((extra,), jnp.int32)], axis=0)
     slot_request, slot_position = slot_layout(block_of_shard[0], cache_keys.shape[0], cached_len)
-    key_request = jnp.concatenate([slot_request, my_request], axis=0)
-    key_position = jnp.concatenate([slot_position, my_position], axis=0)
     gathered = lax.all_gather(
         lax.all_gather(queries, SEQ[1], axis=0, tiled=True), SEQ[0], axis=0, tiled=True
     )
-
-    def block_partial(block_item):
-        q_rows, q_request, q_position = block_item
-        row_count = q_rows.shape[0]
-        q_four = q_rows.reshape(row_count, kv_heads, head_groups, HD)
-        scores = jnp.einsum(
-            "bcgd,kcd->bcgk", q_four, key_block, preferred_element_type=jnp.float32
-        ) * HD ** (-0.5)
-        visible = (q_request[:, None] == key_request[None, :]) & (
-            key_position[None, :] <= q_position[:, None]
-        )
-        visible = visible[:, None, None, :]
-        scores = jnp.where(visible, scores, NEGATIVE)
-        row_top = jnp.max(scores, axis=-1)
-        weights = jnp.where(visible, jnp.exp(scores - row_top[..., None]), 0.0)
-        denominator = jnp.sum(weights, axis=-1)
-        numerator = jnp.einsum(
-            "bcgk,kcd->bcgd",
-            weights.astype(jnp.bfloat16),
-            value_block,
-            preferred_element_type=jnp.float32,
-        )
-        return (
-            row_top.reshape(row_count, q_heads),
-            numerator.reshape(row_count, q_heads, HD),
-            denominator.reshape(row_count, q_heads),
-        )
-
-    def prefill_block(block_item):
-        return block_partial(block_item)
-
-    prefill_parts = lax.map(
-        prefill_block,
-        (
-            gathered[:boundary].reshape(PREFILLS, SPAN, q_heads * HD),
-            request_all[:boundary].reshape(PREFILLS, SPAN),
-            position_all[:boundary].reshape(PREFILLS, SPAN),
-        ),
-    )
-    decode_parts = block_partial(
-        (gathered[boundary:], request_all[boundary:], position_all[boundary:])
-    )
-    row_top = jnp.concatenate(
-        [prefill_parts[0].reshape(boundary, q_heads), decode_parts[0]], axis=0
-    )
-    numerator = jnp.concatenate(
-        [prefill_parts[1].reshape(boundary, q_heads, HD), decode_parts[1]], axis=0
-    )
-    denominator = jnp.concatenate(
-        [prefill_parts[2].reshape(boundary, q_heads), decode_parts[2]], axis=0
+    average, log_weight = attend(
+        gathered, request_all, position_all, cache_keys, cache_values, slot_request, slot_position,
+        new_k, new_v, new_req, new_pos,
     )
     pairs = tok_rows * q_heads
-    seen = denominator > 0
-    average = numerator / jnp.maximum(denominator, 1.0)[..., None]
-    log_weight = jnp.where(seen, row_top + jnp.log(jnp.where(seen, denominator, 1.0)), NEGATIVE)
     high = lax.reduce_precision(log_weight, exponent_bits=8, mantissa_bits=7)
     rest = log_weight - high
     middle = lax.reduce_precision(rest, exponent_bits=8, mantissa_bits=7)

time: 139 us -> 130 us (0.935)
  Pallas kernels: 0 us -> 14.9 us
  matrix products: 15.2 us -> 3.07 us
  other arithmetic: 16 us -> 9.06 us
  local copies, waits for them, and re-layouts: 11.5 us -> 6.79 us
    pallas_call x0 -> x1, Pallas kernels: none -> 14.9 us  [attend(): pl.pallas_call(functools.partial(attend_kernel, heads=heads), grid=grid,...]
    dot_general x6 -> x0, matrix products: 12.1 us -> none  [the longest x3 6.63 us: block_partial(): jnp.einsum('bcgk,kcd->bcgd', weights.astype(jnp.bfloat16), value_block, p...]
    convert_element_type x2 -> x0, local copies, waits for them, and re-layouts: 4.86 us -> none  [per_device(): average.astype(jnp.bfloat16).reshape(seq_count, pairs * HD)]
    reduce_sum x4 -> x1, other arithmetic: 5.14 us -> 0.79 us  [slot_layout(): places = packed - jnp.sum(jnp.where(before, cached_len[None, :], 0), axis=1)]
    and x3 -> x0, other arithmetic: 3.27 us -> none  [block_partial(): (q_request[:, None] == key_request[None, :]) & (key_position[None, :] <=...]
    reshape x2 -> x6, local copies, waits for them, and re-layouts: 0.02 us -> 2.26 us  [the longest x1 0.61 us: per_device(): average.astype(jnp.bfloat16).reshape(seq_count, pairs * HD)]
    concatenate x4 -> x0, other arithmetic: 1.94 us -> none  [the longest x1 1.92 us: per_device(): jnp.concatenate([cache_keys.reshape(-1, kv_heads, HD), new_keys], axis=0)]
    unnamed x32 -> x20, local copies, waits for them, and re-layouts: 3.37 us -> 2.62 us
where the time goes in v5:
time: 130 us
  blocking collectives  64.2 us (49%)
  waiting for transfers between devices  21.5 us (17%)
  Pallas kernels  14.9 us (11%)
  starting transfers between devices  9.15 us (7%)
  other arithmetic  9.06 us (7%)
  local copies, waits for them, and re-layouts  6.79 us (5%)
  matrix products  3.07 us (2%)
    all_gather x1, blocking collectives, per_device(): lax.all_gather(queries, SEQ[1], axis=0, tiled=True)  30.2 us
    all_to_all x1, blocking collectives, per_device(): blocks = lax.all_to_all(blocks, 'tp', 0, 0, tiled=True)  22.6 us
    all_to_all x1, waiting for transfers between devices, per_device(): received = lax.all_to_all(packed, SEQ, 0, 0, tiled=True)  21.5 us
    pallas_call x1, Pallas kernels, attend(): pl.pallas_call(functools.partial(attend_kernel, heads=heads), grid=grid,...  14.9 us
    all_gather x1, blocking collectives, per_device(): lax.all_gather(lax.all_gather(queries, SEQ[1], axis=0, tiled=True), SEQ[0...  11.4 us
    all_to_all x1, starting transfers between devices, per_device(): received = lax.all_to_all(packed, SEQ, 0, 0, tiled=True)  9.15 us
    unnamed x20, local copies, waits for them, and re-layouts  2.62 us
  transfers between devices with their start and end apart: 1, of which 1 were waited for; matrix products, arithmetic and copies ran while one was open for 0% of the time, Pallas kernels for 0%

profile of v5, /device:TPU:1, one launch (start us, length us, event | category | flops | bytes accessed | tf_op | source)
XLA Modules:
  0.0 129.6 jit_solution(168521676178512517)
XLA Ops:
  0.1 0.8 convert_element_type.52
  0.8 1.0 fusion.15
  1.9 1.6 %fusion.45 = f32[17,256]{1,0:T(8,128)S(1)} fusion(bf16[2048,256]{1,0:T(8,128)(2,1)} %param.12, bf16[17,2048]{1,0:T(8,128)(2,1)} %param.10, f32[2048]{0:T(1024)S(1)} %convert_element_type.52, f32[17]{0:T(128)S(1)} %add_rsqrt_fusion), kind=kOutput, calls=%fused_computation.97 | convolution fusion | flops 17965056 | bytes 1143876 | tf_op jit(solution)/shard_map/dot_general | solution.py:155
  3.5 0.1 select_reduce_fusion
  3.6 0.1 dynamic_slice.7
  3.7 1.1 fusion.6
  4.8 0.1 fusion.49
  4.9 0.1 multiply_cosine_fusion.1
  5.0 0.1 subtract_convert_fusion
  5.1 0.1 pad_maximum_fusion
  5.3 30.2 %all-gather = bf16[16,17,256]{2,1,0:T(8,128)(2,1)S(1)} all-gather(bf16[1,17,256]{2,1,0:T(8,128)(2,1)S(1)} %reshape.327), channel_id=1, replica_groups=mesh['seq_hi'=4,'seq_lo'=16,'tp'=8] {'seq_lo'}, dimensions={0}, use_global_device_ids=true | all-gather | bytes 147968 | tf_op jit(solution)/shard_map/all_gather | solution.py:179
  35.4 0.1 reshape.328
  35.5 11.4 %all_gather.7.q_ref = bf16[1088,256]{1,0:T(8,128)(2,1)} all-gather(bf16[272,256]{1,0:T(8,128)(2,1)S(1)} %reshape.328), channel_id=1, replica_groups=mesh['seq_hi'=4,'seq_lo'=16,'tp'=8] {'seq_hi'}, dimensions={0}, use_global_device_ids=true | all-gather | bytes 696320 | tf_op jit(solution)/shard_map/all_gather | solution.py:178
  46.9 0.2 convolution_bitcast_fusion
  47.1 0.1 fusion.41
  47.3 0.6 pad_bitcast_fusion.np_ref
  47.9 0.5 pad_bitcast_fusion.1.nr_ref
  48.4 0.2 convolution_convert_fusion.1
  49.3 0.1 copy.25
  49.4 0.1 reduce-window.8
  49.5 0.1 reduce.2
  49.6 0.8 fusion.8
  50.4 0.6 add_subtract_fusion.kp_ref
  51.0 0.7 fusion.20.nk_ref
  51.7 0.6 concatenate.35.nv_ref
  52.3 14.9 %shard_map.100 = (bf16[1088,256]{1,0:T(8,128)(2,1)}, f32[1088,2]{1,0:T(8,128)}) custom-call(bf16[1088,256]{1,0:T(8,128)(2,1)} %all_gather.7.q_ref, s32[1088,1]{1,0:T(8,128)} %get-tuple-element.26.qr_ref, s32[1088,1]{1,0:T(8,128)} %get-tuple-element.27.qp_ref, bf16[2048,128]{1,0:T(8,128)(2,1)} %k_ref.1, bf16[2048,128]{1,0:T(8,128)(2,1)} %v_ref.1, ...), custom_call_target="tpu_custom_call" | custom-call | tf_op jit(solution)/shard_map/pallas_call | solution.py:98
  67.3 1.3 fusion.12
  68.5 0.2 reshape.318
  68.7 0.2 reshape.319
  68.9 0.2 reshape.320
  69.1 0.6 reshape.317
  69.7 0.3 concatenate.38
  70.0 0.5 broadcast.290
  70.5 1.0 reduce.3
  71.5 1.5 %reshape.332 = bf16[64,2,2227]{2,1,0:T(2,128)(2,1)} reshape(bf16[64,4454]{1,0:T(8,128)(2,1)S(1)} %reduce.3) | data formatting | bytes 1140224
  73.0 9.1 %all-to-all-start = ((bf16[64,2,2227]{2,1,0:T(2,128)(2,1)}), bf16[64,2,2227]{2,1,0:T(2,128)(2,1)S(1)}, u32[]{:S(2)}, u32[]{:S(2)}) async-start(bf16[64,2,2227]{2,1,0:T(2,128)(2,1)} %reshape.332), calls=%async_computation | async-start | bytes 1179648 | tf_op jit(solution)/shard_map/all_to_all | solution.py:199
  82.1 21.5 %all-to-all-done = bf16[64,2,2227]{2,1,0:T(2,128)(2,1)S(1)} async-done(((bf16[64,2,2227]{2,1,0:T(2,128)(2,1)}), bf16[64,2,2227]{2,1,0:T(2,128)(2,1)S(1)}, u32[]{:S(2)}, u32[]{:S(2)}) %all-to-all-start) | async-done | bytes 570144 | tf_op jit(solution)/shard_map/all_to_all | solution.py:199
  103.7 0.9 reshape.333
  104.5 0.1 copy.34
  104.6 0.1 copy.27
  104.7 0.1 fusion.47
  104.9 0.2 fusion.26
  105.0 0.1 div.52
  105.1 0.1 div.53
  105.3 0.8 fusion.4
  106.1 0.2 convolution_convert_fusion
  106.4 22.6 %all_to_all.17 = bf16[8,17,256]{2,1,0:T(8,128)(2,1)S(1)} all-to-all(bf16[8,17,256]{2,1,0:T(8,128)(2,1)S(1)} %bitcast.44), channel_id=1, replica_groups=mesh['seq_hi'=4,'seq_lo'=16,'tp'=8] {'tp'}, dimensions={0} | all-to-all | bytes 139264 | tf_op jit(solution)/shard_map/all_to_all | solution.py:218
  129.0 0.6 reduce_sum.78
  (29 shorter events, 0.2 us)
Async XLA Ops:
  0.0 106.1 %copy-start = (bf16[256,2048]{1,0:T(8,128)(2,1)S(1)}, bf16[256,2048]{1,0:T(8,128)(2,1)}, u32[]{:S(2)}) copy-start(bf16[256,2048]{1,0:T(8,128)(2,1)} %param.15) | copy-start | bytes 3145732
  0.0 3.5 %copy-start.5 = (s32[66]{0:T(128)S(1)}, s32[66]{0:T(128)}, u32[]{:S(2)}) copy-start(s32[66]{0:T(128)} %param.18) | copy-start | bytes 796
  3.7 43.2 %copy-start.1 = (bf16[17,2048]{1,0:T(8,128)(2,1)S(1)}, bf16[17,2048]{1,0:T(8,128)(2,1)}, u32[]{:S(2)}) copy-start(bf16[17,2048]{1,0:T(8,128)(2,1)} %param.10) | copy-start | bytes 208900
  3.7 43.2 %copy-start.3 = (bf16[2048,128]{1,0:T(8,128)(2,1)S(1)}, bf16[2048,128]{1,0:T(8,128)(2,1)}, u32[]{:S(2)}) copy-start(bf16[2048,128]{1,0:T(8,128)(2,1)} %param.13) | copy-start | bytes 1572868
  4.8 43.6 %copy-start.4 = (bf16[2048,128]{1,0:T(8,128)(2,1)S(1)}, bf16[2048,128]{1,0:T(8,128)(2,1)}, u32[]{:S(2)}) copy-start(bf16[2048,128]{1,0:T(8,128)(2,1)} %param.14) | copy-start | bytes 1572868
  67.3 1.8 %copy-start.2 = (bf16[1088,256]{1,0:T(8,128)(2,1)S(1)}, bf16[1088,256]{1,0:T(8,128)(2,1)}, u32[]{:S(2)}) copy-start(bf16[1088,256]{1,0:T(8,128)(2,1)} %get-tuple-element.7) | copy-start | bytes 1671172
  73.0 30.7 %all-to-all-start = ((bf16[64,2,2227]{2,1,0:T(2,128)(2,1)}), bf16[64,2,2227]{2,1,0:T(2,128)(2,1)S(1)}, u32[]{:S(2)}, u32[]{:S(2)}) async-start(bf16[64,2,2227]{2,1,0:T(2,128)(2,1)} %reshape.332), calls=%async_computation | async-start | bytes 1179648 | tf_op jit(solution)/shard_map/all_to_all | solution.py:199

commit v6 on v5

--- a/solution.py
+++ b/solution.py
@@ -56,7 +56,7 @@
     q_ref, qr_ref, qp_ref, k_ref, v_ref, kr_ref, kp_ref, nk_ref, nv_ref, nr_ref, np_ref,
     avg_ref, lw_ref, *, heads
 ):
-    seen_cache = (qr_ref[...] == kr_ref[...]) & (kp_ref[...] <= qp_ref[...])
+    seen_cache = qr_ref[...] == kr_ref[...]
     seen_new = (qr_ref[...] == nr_ref[...]) & (np_ref[...] <= qp_ref[...])
     tops = []
     for g in range(heads):

time: 130 us -> 129 us (level)
  no operation moved by 1% of the time
where the time goes in v6:
time: 129 us
  blocking collectives  64.2 us (50%)
  waiting for transfers between devices  21.5 us (17%)
  Pallas kernels  14 us (11%)
  starting transfers between devices  9.16 us (7%)
  other arithmetic  9.06 us (7%)
  local copies, waits for them, and re-layouts  6.79 us (5%)
  matrix products  3.07 us (2%)
    all_gather x1, blocking collectives, per_device(): lax.all_gather(queries, SEQ[1], axis=0, tiled=True)  30.2 us
    all_to_all x1, blocking collectives, per_device(): blocks = lax.all_to_all(blocks, 'tp', 0, 0, tiled=True)  22.6 us
    all_to_all x1, waiting for transfers between devices, per_device(): received = lax.all_to_all(packed, SEQ, 0, 0, tiled=True)  21.5 us
    pallas_call x1, Pallas kernels, attend(): pl.pallas_call(functools.partial(attend_kernel, heads=heads), grid=grid,...  14 us
    all_gather x1, blocking collectives, per_device(): lax.all_gather(lax.all_gather(queries, SEQ[1], axis=0, tiled=True), SEQ[0...  11.4 us
    all_to_all x1, starting transfers between devices, per_device(): received = lax.all_to_all(packed, SEQ, 0, 0, tiled=True)  9.16 us
    unnamed x20, local copies, waits for them, and re-layouts  2.62 us
  transfers between devices with their start and end apart: 1, of which 1 were waited for; matrix products, arithmetic and copies ran while one was open for 0% of the time, Pallas kernels for 0%

profile of v6, /device:TPU:1, one launch (start us, length us, event | category | flops | bytes accessed | tf_op | source)
XLA Modules:
  0.0 128.8 jit_solution(12725887681197523097)
XLA Ops:
  0.1 0.8 convert_element_type.52
  0.8 1.0 fusion.15
  1.9 1.6 %fusion.45 = f32[17,256]{1,0:T(8,128)S(1)} fusion(bf16[2048,256]{1,0:T(8,128)(2,1)} %param.12, bf16[17,2048]{1,0:T(8,128)(2,1)} %param.10, f32[2048]{0:T(1024)S(1)} %convert_element_type.52, f32[17]{0:T(128)S(1)} %add_rsqrt_fusion), kind=kOutput, calls=%fused_computation.97 | convolution fusion | flops 17965056 | bytes 1143876 | tf_op jit(solution)/shard_map/dot_general | solution.py:155
  3.5 0.1 select_reduce_fusion
  3.6 0.1 dynamic_slice.7
  3.7 1.1 fusion.6
  4.8 0.1 fusion.49
  4.9 0.1 multiply_cosine_fusion.1
  5.0 0.1 subtract_convert_fusion
  5.1 0.1 pad_maximum_fusion
  5.3 30.2 %all-gather = bf16[16,17,256]{2,1,0:T(8,128)(2,1)S(1)} all-gather(bf16[1,17,256]{2,1,0:T(8,128)(2,1)S(1)} %reshape.327), channel_id=1, replica_groups=mesh['seq_hi'=4,'seq_lo'=16,'tp'=8] {'seq_lo'}, dimensions={0}, use_global_device_ids=true | all-gather | bytes 147968 | tf_op jit(solution)/shard_map/all_gather | solution.py:179
  35.4 0.1 reshape.328
  35.5 11.4 %all_gather.7.q_ref = bf16[1088,256]{1,0:T(8,128)(2,1)} all-gather(bf16[272,256]{1,0:T(8,128)(2,1)S(1)} %reshape.328), channel_id=1, replica_groups=mesh['seq_hi'=4,'seq_lo'=16,'tp'=8] {'seq_hi'}, dimensions={0}, use_global_device_ids=true | all-gather | bytes 696320 | tf_op jit(solution)/shard_map/all_gather | solution.py:178
  46.9 0.2 convolution_bitcast_fusion
  47.1 0.1 fusion.41
  47.3 0.6 pad_bitcast_fusion.np_ref
  47.9 0.5 pad_bitcast_fusion.1.nr_ref
  48.4 0.2 convolution_convert_fusion.1
  49.3 0.1 copy.25
  49.4 0.1 reduce-window.8
  49.5 0.1 reduce.2
  49.6 0.8 fusion.8
  50.4 0.6 add_subtract_fusion.kp_ref
  51.0 0.7 fusion.20.nk_ref
  51.7 0.6 concatenate.35.nv_ref
  52.3 14.0 %shard_map.100 = (bf16[1088,256]{1,0:T(8,128)(2,1)}, f32[1088,2]{1,0:T(8,128)}) custom-call(bf16[1088,256]{1,0:T(8,128)(2,1)} %all_gather.7.q_ref, s32[1088,1]{1,0:T(8,128)} %get-tuple-element.26.qr_ref, s32[1088,1]{1,0:T(8,128)} %get-tuple-element.27.qp_ref, bf16[2048,128]{1,0:T(8,128)(2,1)} %k_ref.1, bf16[2048,128]{1,0:T(8,128)(2,1)} %v_ref.1, ...), custom_call_target="tpu_custom_call" | custom-call | tf_op jit(solution)/shard_map/pallas_call | solution.py:98
  66.4 1.3 fusion.12
  67.7 0.2 reshape.318
  67.8 0.2 reshape.319
  68.0 0.2 reshape.320
  68.2 0.6 reshape.317
  68.8 0.3 concatenate.38
  69.1 0.5 broadcast.290
  69.6 1.0 reduce.3
  70.6 1.5 %reshape.332 = bf16[64,2,2227]{2,1,0:T(2,128)(2,1)} reshape(bf16[64,4454]{1,0:T(8,128)(2,1)S(1)} %reduce.3) | data formatting | bytes 1140224
  72.1 9.2 %all-to-all-start = ((bf16[64,2,2227]{2,1,0:T(2,128)(2,1)}), bf16[64,2,2227]{2,1,0:T(2,128)(2,1)S(1)}, u32[]{:S(2)}, u32[]{:S(2)}) async-start(bf16[64,2,2227]{2,1,0:T(2,128)(2,1)} %reshape.332), calls=%async_computation | async-start | bytes 1179648 | tf_op jit(solution)/shard_map/all_to_all | solution.py:199
  81.3 21.5 %all-to-all-done = bf16[64,2,2227]{2,1,0:T(2,128)(2,1)S(1)} async-done(((bf16[64,2,2227]{2,1,0:T(2,128)(2,1)}), bf16[64,2,2227]{2,1,0:T(2,128)(2,1)S(1)}, u32[]{:S(2)}, u32[]{:S(2)}) %all-to-all-start) | async-done | bytes 570144 | tf_op jit(solution)/shard_map/all_to_all | solution.py:199
  102.8 0.9 reshape.333
  103.7 0.1 copy.34
  103.8 0.1 copy.27
  103.9 0.1 fusion.47
  104.0 0.2 fusion.26
  104.2 0.1 div.52
  104.3 0.1 div.53
  104.4 0.8 fusion.4
  105.2 0.2 convolution_convert_fusion
  105.5 22.6 %all_to_all.17 = bf16[8,17,256]{2,1,0:T(8,128)(2,1)S(1)} all-to-all(bf16[8,17,256]{2,1,0:T(8,128)(2,1)S(1)} %bitcast.44), channel_id=1, replica_groups=mesh['seq_hi'=4,'seq_lo'=16,'tp'=8] {'tp'}, dimensions={0} | all-to-all | bytes 139264 | tf_op jit(solution)/shard_map/all_to_all | solution.py:218
  128.1 0.6 reduce_sum.78
  (29 shorter events, 0.2 us)
Async XLA Ops:
  0.0 105.2 %copy-start = (bf16[256,2048]{1,0:T(8,128)(2,1)S(1)}, bf16[256,2048]{1,0:T(8,128)(2,1)}, u32[]{:S(2)}) copy-start(bf16[256,2048]{1,0:T(8,128)(2,1)} %param.15) | copy-start | bytes 3145732
  0.0 3.5 %copy-start.5 = (s32[66]{0:T(128)S(1)}, s32[66]{0:T(128)}, u32[]{:S(2)}) copy-start(s32[66]{0:T(128)} %param.18) | copy-start | bytes 796
  3.7 43.2 %copy-start.1 = (bf16[17,2048]{1,0:T(8,128)(2,1)S(1)}, bf16[17,2048]{1,0:T(8,128)(2,1)}, u32[]{:S(2)}) copy-start(bf16[17,2048]{1,0:T(8,128)(2,1)} %param.10) | copy-start | bytes 208900
  3.7 43.2 %copy-start.3 = (bf16[2048,128]{1,0:T(8,128)(2,1)S(1)}, bf16[2048,128]{1,0:T(8,128)(2,1)}, u32[]{:S(2)}) copy-start(bf16[2048,128]{1,0:T(8,128)(2,1)} %param.13) | copy-start | bytes 1572868
  4.8 43.6 %copy-start.4 = (bf16[2048,128]{1,0:T(8,128)(2,1)S(1)}, bf16[2048,128]{1,0:T(8,128)(2,1)}, u32[]{:S(2)}) copy-start(bf16[2048,128]{1,0:T(8,128)(2,1)} %param.14) | copy-start | bytes 1572868
  66.4 1.8 %copy-start.2 = (bf16[1088,256]{1,0:T(8,128)(2,1)S(1)}, bf16[1088,256]{1,0:T(8,128)(2,1)}, u32[]{:S(2)}) copy-start(bf16[1088,256]{1,0:T(8,128)(2,1)} %get-tuple-element.7) | copy-start | bytes 1671172
  72.1 30.7 %all-to-all-start = ((bf16[64,2,2227]{2,1,0:T(2,128)(2,1)}), bf16[64,2,2227]{2,1,0:T(2,128)(2,1)S(1)}, u32[]{:S(2)}, u32[]{:S(2)}) async-start(bf16[64,2,2227]{2,1,0:T(2,128)(2,1)} %reshape.332), calls=%async_computation | async-start | bytes 1179648 | tf_op jit(solution)/shard_map/all_to_all | solution.py:199

commit v7 on v6

--- a/solution.py
+++ b/solution.py
@@ -87,7 +87,7 @@
     lw_ref[...] = jnp.concatenate(tops, axis=1)
 
 
-def attend(q, q_req, q_pos, keys, values, k_req, k_pos, new_k, new_v, n_req, n_pos, block_rows=136):
+def attend(q, q_req, q_pos, keys, values, k_req, k_pos, new_k, new_v, n_req, n_pos, block_rows=272):
     rows, width = q.shape
     heads = width // HD
     slots = keys.shape[0]

time: 129 us -> 129 us (level)
  no operation moved by 1% of the time
where the time goes in v7:
time: 129 us; the launch traced here: 128 us
  blocking collectives  64.2 us (50%)
  waiting for transfers between devices  21.5 us (17%)
  Pallas kernels  13.6 us (11%)
  starting transfers between devices  9.15 us (7%)
  other arithmetic  9.06 us (7%)
  local copies, waits for them, and re-layouts  6.79 us (5%)
  matrix products  3.07 us (2%)
    all_gather x1, blocking collectives, per_device(): lax.all_gather(queries, SEQ[1], axis=0, tiled=True)  30.2 us
    all_to_all x1, blocking collectives, per_device(): blocks = lax.all_to_all(blocks, 'tp', 0, 0, tiled=True)  22.6 us
    all_to_all x1, waiting for transfers between devices, per_device(): received = lax.all_to_all(packed, SEQ, 0, 0, tiled=True)  21.5 us
    pallas_call x1, Pallas kernels, attend(): pl.pallas_call(functools.partial(attend_kernel, heads=heads), grid=grid,...  13.6 us
    all_gather x1, blocking collectives, per_device(): lax.all_gather(lax.all_gather(queries, SEQ[1], axis=0, tiled=True), SEQ[0...  11.4 us
    all_to_all x1, starting transfers between devices, per_device(): received = lax.all_to_all(packed, SEQ, 0, 0, tiled=True)  9.15 us
    unnamed x20, local copies, waits for them, and re-layouts  2.62 us
  transfers between devices with their start and end apart: 1, of which 1 were waited for; matrix products, arithmetic and copies ran while one was open for 0% of the time, Pallas kernels for 0%

profile of v7, /device:TPU:1, one launch (start us, length us, event | category | flops | bytes accessed | tf_op | source)
XLA Modules:
  0.0 128.3 jit_solution(17112088652837208518)
XLA Ops:
  0.1 0.8 convert_element_type.52
  0.8 1.0 fusion.15
  1.9 1.6 %fusion.45 = f32[17,256]{1,0:T(8,128)S(1)} fusion(bf16[2048,256]{1,0:T(8,128)(2,1)} %param.12, bf16[17,2048]{1,0:T(8,128)(2,1)} %param.10, f32[2048]{0:T(1024)S(1)} %convert_element_type.52, f32[17]{0:T(128)S(1)} %add_rsqrt_fusion), kind=kOutput, calls=%fused_computation.97 | convolution fusion | flops 17965056 | bytes 1143876 | tf_op jit(solution)/shard_map/dot_general | solution.py:155
  3.5 0.1 select_reduce_fusion
  3.6 0.1 dynamic_slice.7
  3.7 1.1 fusion.6
  4.8 0.1 fusion.49
  4.9 0.1 multiply_cosine_fusion.1
  5.0 0.1 subtract_convert_fusion
  5.1 0.1 pad_maximum_fusion
  5.3 30.2 %all-gather = bf16[16,17,256]{2,1,0:T(8,128)(2,1)S(1)} all-gather(bf16[1,17,256]{2,1,0:T(8,128)(2,1)S(1)} %reshape.327), channel_id=1, replica_groups=mesh['seq_hi'=4,'seq_lo'=16,'tp'=8] {'seq_lo'}, dimensions={0}, use_global_device_ids=true | all-gather | bytes 147968 | tf_op jit(solution)/shard_map/all_gather | solution.py:179
  35.4 0.1 reshape.328
  35.5 11.4 %all_gather.7.q_ref = bf16[1088,256]{1,0:T(8,128)(2,1)} all-gather(bf16[272,256]{1,0:T(8,128)(2,1)S(1)} %reshape.328), channel_id=1, replica_groups=mesh['seq_hi'=4,'seq_lo'=16,'tp'=8] {'seq_hi'}, dimensions={0}, use_global_device_ids=true | all-gather | bytes 696320 | tf_op jit(solution)/shard_map/all_gather | solution.py:178
  46.9 0.2 convolution_bitcast_fusion
  47.1 0.1 fusion.41
  47.3 0.6 pad_bitcast_fusion.np_ref
  47.9 0.5 pad_bitcast_fusion.1.nr_ref
  48.4 0.2 convolution_convert_fusion.1
  49.3 0.1 copy.25
  49.4 0.1 reduce-window.8
  49.5 0.1 reduce.2
  49.6 0.8 fusion.8
  50.4 0.6 add_subtract_fusion.kp_ref
  51.0 0.7 fusion.20.nk_ref
  51.7 0.6 concatenate.35.nv_ref
  52.3 13.6 %shard_map.100 = (bf16[1088,256]{1,0:T(8,128)(2,1)}, f32[1088,2]{1,0:T(8,128)}) custom-call(bf16[1088,256]{1,0:T(8,128)(2,1)} %all_gather.7.q_ref, s32[1088,1]{1,0:T(8,128)} %get-tuple-element.26.qr_ref, s32[1088,1]{1,0:T(8,128)} %get-tuple-element.27.qp_ref, bf16[2048,128]{1,0:T(8,128)(2,1)} %k_ref.1, bf16[2048,128]{1,0:T(8,128)(2,1)} %v_ref.1, ...), custom_call_target="tpu_custom_call" | custom-call | tf_op jit(solution)/shard_map/pallas_call | solution.py:98
  65.9 1.3 fusion.12
  67.2 0.2 reshape.318
  67.4 0.2 reshape.319
  67.6 0.2 reshape.320
  67.8 0.6 reshape.317
  68.4 0.3 concatenate.38
  68.6 0.5 broadcast.290
  69.2 1.0 reduce.3
  70.1 1.5 %reshape.332 = bf16[64,2,2227]{2,1,0:T(2,128)(2,1)} reshape(bf16[64,4454]{1,0:T(8,128)(2,1)S(1)} %reduce.3) | data formatting | bytes 1140224
  71.6 9.1 %all-to-all-start = ((bf16[64,2,2227]{2,1,0:T(2,128)(2,1)}), bf16[64,2,2227]{2,1,0:T(2,128)(2,1)S(1)}, u32[]{:S(2)}, u32[]{:S(2)}) async-start(bf16[64,2,2227]{2,1,0:T(2,128)(2,1)} %reshape.332), calls=%async_computation | async-start | bytes 1179648 | tf_op jit(solution)/shard_map/all_to_all | solution.py:199
  80.8 21.5 %all-to-all-done = bf16[64,2,2227]{2,1,0:T(2,128)(2,1)S(1)} async-done(((bf16[64,2,2227]{2,1,0:T(2,128)(2,1)}), bf16[64,2,2227]{2,1,0:T(2,128)(2,1)S(1)}, u32[]{:S(2)}, u32[]{:S(2)}) %all-to-all-start) | async-done | bytes 570144 | tf_op jit(solution)/shard_map/all_to_all | solution.py:199
  102.3 0.9 reshape.333
  103.2 0.1 copy.34
  103.3 0.1 copy.27
  103.4 0.1 fusion.47
  103.5 0.2 fusion.26
  103.7 0.1 div.52
  103.8 0.1 div.53
  103.9 0.8 fusion.4
  104.7 0.2 convolution_convert_fusion
  105.0 22.6 %all_to_all.17 = bf16[8,17,256]{2,1,0:T(8,128)(2,1)S(1)} all-to-all(bf16[8,17,256]{2,1,0:T(8,128)(2,1)S(1)} %bitcast.44), channel_id=1, replica_groups=mesh['seq_hi'=4,'seq_lo'=16,'tp'=8] {'tp'}, dimensions={0} | all-to-all | bytes 139264 | tf_op jit(solution)/shard_map/all_to_all | solution.py:218
  127.7 0.6 reduce_sum.78
  (29 shorter events, 0.2 us)
Async XLA Ops:
  0.0 104.7 %copy-start = (bf16[256,2048]{1,0:T(8,128)(2,1)S(1)}, bf16[256,2048]{1,0:T(8,128)(2,1)}, u32[]{:S(2)}) copy-start(bf16[256,2048]{1,0:T(8,128)(2,1)} %param.15) | copy-start | bytes 3145732
  0.0 3.5 %copy-start.5 = (s32[66]{0:T(128)S(1)}, s32[66]{0:T(128)}, u32[]{:S(2)}) copy-start(s32[66]{0:T(128)} %param.18) | copy-start | bytes 796
  3.7 43.2 %copy-start.1 = (bf16[17,2048]{1,0:T(8,128)(2,1)S(1)}, bf16[17,2048]{1,0:T(8,128)(2,1)}, u32[]{:S(2)}) copy-start(bf16[17,2048]{1,0:T(8,128)(2,1)} %param.10) | copy-start | bytes 208900
  3.7 43.2 %copy-start.3 = (bf16[2048,128]{1,0:T(8,128)(2,1)S(1)}, bf16[2048,128]{1,0:T(8,128)(2,1)}, u32[]{:S(2)}) copy-start(bf16[2048,128]{1,0:T(8,128)(2,1)} %param.13) | copy-start | bytes 1572868
  4.8 43.6 %copy-start.4 = (bf16[2048,128]{1,0:T(8,128)(2,1)S(1)}, bf16[2048,128]{1,0:T(8,128)(2,1)}, u32[]{:S(2)}) copy-start(bf16[2048,128]{1,0:T(8,128)(2,1)} %param.14) | copy-start | bytes 1572868
  65.9 1.8 %copy-start.2 = (bf16[1088,256]{1,0:T(8,128)(2,1)S(1)}, bf16[1088,256]{1,0:T(8,128)(2,1)}, u32[]{:S(2)}) copy-start(bf16[1088,256]{1,0:T(8,128)(2,1)} %get-tuple-element.7) | copy-start | bytes 1671172
  71.6 30.7 %all-to-all-start = ((bf16[64,2,2227]{2,1,0:T(2,128)(2,1)}), bf16[64,2,2227]{2,1,0:T(2,128)(2,1)S(1)}, u32[]{:S(2)}, u32[]{:S(2)}) async-start(bf16[64,2,2227]{2,1,0:T(2,128)(2,1)} %reshape.332), calls=%async_computation | async-start | bytes 1179648 | tf_op jit(solution)/shard_map/all_to_all | solution.py:199

commit v8 on v7

--- a/solution.py
+++ b/solution.py
@@ -193,12 +193,13 @@
             high.astype(jnp.bfloat16).reshape(seq_count, pairs),
             middle.astype(jnp.bfloat16).reshape(seq_count, pairs),
             low.astype(jnp.bfloat16).reshape(seq_count, pairs),
+            jnp.zeros((seq_count, -(-pairs * (HD + 3) // 256) * 256 - pairs * (HD + 3)), jnp.bfloat16),
         ],
         axis=1,
     )
     received = lax.all_to_all(packed, SEQ, 0, 0, tiled=True)
     part_avg = received[:, : pairs * HD].astype(jnp.float32)
-    tail = received[:, pairs * HD :].astype(jnp.float32).reshape(seq_count, 3, pairs)
+    tail = received[:, pairs * HD : pairs * (HD + 3)].astype(jnp.float32).reshape(seq_count, 3, pairs)
     part_log = tail[:, 0] + (tail[:, 1] + tail[:, 2])
     overall = jnp.max(part_log, axis=0, keepdims=True)
     factor = jnp.exp(part_log - overall)

time: 129 us -> 128 us (level)
  no operation moved by 1% of the time
where the time goes in v8:
time: 128 us; the launch traced here: 127 us
  blocking collectives  64.2 us (50%)
  waiting for transfers between devices  21.5 us (17%)
  Pallas kernels  13.6 us (11%)
  starting transfers between devices  9.15 us (7%)
  other arithmetic  9.14 us (7%)
  local copies, waits for them, and re-layouts  5.84 us (5%)
  matrix products  3.07 us (2%)
    all_gather x1, blocking collectives, per_device(): lax.all_gather(queries, SEQ[1], axis=0, tiled=True)  30.2 us
    all_to_all x1, blocking collectives, per_device(): blocks = lax.all_to_all(blocks, 'tp', 0, 0, tiled=True)  22.6 us
    all_to_all x1, waiting for transfers between devices, per_device(): received = lax.all_to_all(packed, SEQ, 0, 0, tiled=True)  21.5 us
    pallas_call x1, Pallas kernels, attend(): pl.pallas_call(functools.partial(attend_kernel, heads=heads), grid=grid,...  13.6 us
    all_gather x1, blocking collectives, per_device(): lax.all_gather(lax.all_gather(queries, SEQ[1], axis=0, tiled=True), SEQ[0...  11.4 us
    all_to_all x1, starting transfers between devices, per_device(): received = lax.all_to_all(packed, SEQ, 0, 0, tiled=True)  9.15 us
  transfers between devices with their start and end apart: 1, of which 1 were waited for; matrix products, arithmetic and copies ran while one was open for 0% of the time, Pallas kernels for 0%

profile of v8, /device:TPU:1, one launch (start us, length us, event | category | flops | bytes accessed | tf_op | source)
XLA Modules:
  0.0 127.4 jit_solution(15071061389090022149)
XLA Ops:
  0.1 0.8 convert_element_type.52
  0.8 1.0 fusion.15
  1.9 1.6 %fusion.45 = f32[17,256]{1,0:T(8,128)S(1)} fusion(bf16[2048,256]{1,0:T(8,128)(2,1)} %param.12, bf16[17,2048]{1,0:T(8,128)(2,1)} %param.10, f32[2048]{0:T(1024)S(1)} %convert_element_type.52, f32[17]{0:T(128)S(1)} %add_rsqrt_fusion), kind=kOutput, calls=%fused_computation.97 | convolution fusion | flops 17965056 | bytes 1143876 | tf_op jit(solution)/shard_map/dot_general | solution.py:155
  3.5 0.1 select_reduce_fusion
  3.6 0.1 dynamic_slice.7
  3.7 1.1 fusion.6
  4.8 0.1 fusion.49
  4.9 0.1 multiply_cosine_fusion.1
  5.0 0.1 subtract_convert_fusion
  5.1 0.1 pad_maximum_fusion
  5.3 30.2 %all-gather = bf16[16,17,256]{2,1,0:T(8,128)(2,1)S(1)} all-gather(bf16[1,17,256]{2,1,0:T(8,128)(2,1)S(1)} %reshape.327), channel_id=1, replica_groups=mesh['seq_hi'=4,'seq_lo'=16,'tp'=8] {'seq_lo'}, dimensions={0}, use_global_device_ids=true | all-gather | bytes 147968 | tf_op jit(solution)/shard_map/all_gather | solution.py:179
  35.4 0.1 reshape.328
  35.5 11.4 %all_gather.7.q_ref = bf16[1088,256]{1,0:T(8,128)(2,1)} all-gather(bf16[272,256]{1,0:T(8,128)(2,1)S(1)} %reshape.328), channel_id=1, replica_groups=mesh['seq_hi'=4,'seq_lo'=16,'tp'=8] {'seq_hi'}, dimensions={0}, use_global_device_ids=true | all-gather | bytes 696320 | tf_op jit(solution)/shard_map/all_gather | solution.py:178
  46.9 0.2 convolution_bitcast_fusion
  47.1 0.1 fusion.41
  47.3 0.6 pad_bitcast_fusion.np_ref
  47.9 0.5 pad_bitcast_fusion.1.nr_ref
  48.4 0.2 convolution_convert_fusion.1
  49.3 0.1 copy.25
  49.4 0.1 reduce-window.8
  49.5 0.1 reduce.2
  49.6 0.8 fusion.8
  50.4 0.6 add_subtract_fusion.kp_ref
  51.0 0.7 fusion.20.nk_ref
  51.7 0.6 concatenate.35.nv_ref
  52.3 13.6 %shard_map.100 = (bf16[1088,256]{1,0:T(8,128)(2,1)}, f32[1088,2]{1,0:T(8,128)}) custom-call(bf16[1088,256]{1,0:T(8,128)(2,1)} %all_gather.7.q_ref, s32[1088,1]{1,0:T(8,128)} %get-tuple-element.26.qr_ref, s32[1088,1]{1,0:T(8,128)} %get-tuple-element.27.qp_ref, bf16[2048,128]{1,0:T(8,128)(2,1)} %k_ref.1, bf16[2048,128]{1,0:T(8,128)(2,1)} %v_ref.1, ...), custom_call_target="tpu_custom_call" | custom-call | tf_op jit(solution)/shard_map/pallas_call | solution.py:98
  65.9 1.3 fusion.12
  67.2 0.2 reshape.318
  67.4 0.2 reshape.319
  67.6 0.2 reshape.320
  67.8 0.6 reshape.317
  68.4 0.3 concatenate.38
  68.7 0.5 broadcast.290
  69.2 1.0 reduce.3
  70.2 0.9 reshape.332
  71.2 9.1 %all-to-all-start = ((bf16[64,2,2304]{2,1,0:T(2,128)(2,1)}), bf16[64,2,2304]{2,1,0:T(2,128)(2,1)S(1)}, u32[]{:S(2)}, u32[]{:S(2)}) async-start(bf16[64,2,2304]{2,1,0:T(2,128)(2,1)} %reshape.332), calls=%async_computation | async-start | bytes 1179648 | tf_op jit(solution)/shard_map/all_to_all | solution.py:200
  80.3 21.5 %all-to-all-done = bf16[64,2,2304]{2,1,0:T(2,128)(2,1)S(1)} async-done(((bf16[64,2,2304]{2,1,0:T(2,128)(2,1)}), bf16[64,2,2304]{2,1,0:T(2,128)(2,1)S(1)}, u32[]{:S(2)}, u32[]{:S(2)}) %all-to-all-start) | async-done | bytes 589856 | tf_op jit(solution)/shard_map/all_to_all | solution.py:200
  101.8 0.5 reshape.333
  102.3 0.1 copy.34
  102.4 0.1 copy.27
  102.5 0.1 fusion.47
  102.7 0.2 fusion.26
  102.8 0.1 div.52
  102.9 0.1 div.53
  103.1 0.8 fusion.4
  103.9 0.2 convolution_convert_fusion
  104.2 22.6 %all_to_all.17 = bf16[8,17,256]{2,1,0:T(8,128)(2,1)S(1)} all-to-all(bf16[8,17,256]{2,1,0:T(8,128)(2,1)S(1)} %bitcast.44), channel_id=1, replica_groups=mesh['seq_hi'=4,'seq_lo'=16,'tp'=8] {'tp'}, dimensions={0} | all-to-all | bytes 139264 | tf_op jit(solution)/shard_map/all_to_all | solution.py:219
  126.8 0.6 reduce_sum.78
  (30 shorter events, 0.2 us)
Async XLA Ops:
  0.0 103.9 %copy-start = (bf16[256,2048]{1,0:T(8,128)(2,1)S(1)}, bf16[256,2048]{1,0:T(8,128)(2,1)}, u32[]{:S(2)}) copy-start(bf16[256,2048]{1,0:T(8,128)(2,1)} %param.15) | copy-start | bytes 3145732
  0.0 3.5 %copy-start.5 = (s32[66]{0:T(128)S(1)}, s32[66]{0:T(128)}, u32[]{:S(2)}) copy-start(s32[66]{0:T(128)} %param.18) | copy-start | bytes 796
  3.7 43.2 %copy-start.1 = (bf16[17,2048]{1,0:T(8,128)(2,1)S(1)}, bf16[17,2048]{1,0:T(8,128)(2,1)}, u32[]{:S(2)}) copy-start(bf16[17,2048]{1,0:T(8,128)(2,1)} %param.10) | copy-start | bytes 208900
  3.7 43.2 %copy-start.3 = (bf16[2048,128]{1,0:T(8,128)(2,1)S(1)}, bf16[2048,128]{1,0:T(8,128)(2,1)}, u32[]{:S(2)}) copy-start(bf16[2048,128]{1,0:T(8,128)(2,1)} %param.13) | copy-start | bytes 1572868
  4.8 43.6 %copy-start.4 = (bf16[2048,128]{1,0:T(8,128)(2,1)S(1)}, bf16[2048,128]{1,0:T(8,128)(2,1)}, u32[]{:S(2)}) copy-start(bf16[2048,128]{1,0:T(8,128)(2,1)} %param.14) | copy-start | bytes 1572868
  65.9 1.8 %copy-start.2 = (bf16[1088,256]{1,0:T(8,128)(2,1)S(1)}, bf16[1088,256]{1,0:T(8,128)(2,1)}, u32[]{:S(2)}) copy-start(bf16[1088,256]{1,0:T(8,128)(2,1)} %get-tuple-element.7) | copy-start | bytes 1671172
  71.2 30.7 %all-to-all-start = ((bf16[64,2,2304]{2,1,0:T(2,128)(2,1)}), bf16[64,2,2304]{2,1,0:T(2,128)(2,1)S(1)}, u32[]{:S(2)}, u32[]{:S(2)}) async-start(bf16[64,2,2304]{2,1,0:T(2,128)(2,1)} %reshape.332), calls=%async_computation | async-start | bytes 1179648 | tf_op jit(solution)/shard_map/all_to_all | solution.py:200

commit v9 on v8

--- a/solution.py
+++ b/solution.py
@@ -87,7 +87,7 @@
     lw_ref[...] = jnp.concatenate(tops, axis=1)
 
 
-def attend(q, q_req, q_pos, keys, values, k_req, k_pos, new_k, new_v, n_req, n_pos, block_rows=272):
+def attend(q, q_req, q_pos, keys, values, k_req, k_pos, new_k, new_v, n_req, n_pos, block_rows=544):
     rows, width = q.shape
     heads = width // HD
     slots = keys.shape[0]

time: 128 us -> 127 us (level)
  no operation moved by 1% of the time
where the time goes in v9:
time: 127 us
  blocking collectives  64.2 us (51%)
  waiting for transfers between devices  21.5 us (17%)
  Pallas kernels  12.8 us (10%)
  starting transfers between devices  9.15 us (7%)
  other arithmetic  9.14 us (7%)
  local copies, waits for them, and re-layouts  5.84 us (5%)
  matrix products  3.07 us (2%)
    all_gather x1, blocking collectives, per_device(): lax.all_gather(queries, SEQ[1], axis=0, tiled=True)  30.2 us
    all_to_all x1, blocking collectives, per_device(): blocks = lax.all_to_all(blocks, 'tp', 0, 0, tiled=True)  22.6 us
    all_to_all x1, waiting for transfers between devices, per_device(): received = lax.all_to_all(packed, SEQ, 0, 0, tiled=True)  21.5 us
    pallas_call x1, Pallas kernels, attend(): pl.pallas_call(functools.partial(attend_kernel, heads=heads), grid=grid,...  12.8 us
    all_gather x1, blocking collectives, per_device(): lax.all_gather(lax.all_gather(queries, SEQ[1], axis=0, tiled=True), SEQ[0...  11.4 us
    all_to_all x1, starting transfers between devices, per_device(): received = lax.all_to_all(packed, SEQ, 0, 0, tiled=True)  9.15 us
  transfers between devices with their start and end apart: 1, of which 1 were waited for; matrix products, arithmetic and copies ran while one was open for 0% of the time, Pallas kernels for 0%

profile of v9, /device:TPU:1, one launch (start us, length us, event | category | flops | bytes accessed | tf_op | source)
XLA Modules:
  0.0 126.7 jit_solution(11329638558336671627)
XLA Ops:
  0.1 0.8 convert_element_type.52
  0.8 1.0 fusion.15
  1.9 1.6 %fusion.45 = f32[17,256]{1,0:T(8,128)S(1)} fusion(bf16[2048,256]{1,0:T(8,128)(2,1)} %param.12, bf16[17,2048]{1,0:T(8,128)(2,1)} %param.10, f32[2048]{0:T(1024)S(1)} %convert_element_type.52, f32[17]{0:T(128)S(1)} %add_rsqrt_fusion), kind=kOutput, calls=%fused_computation.97 | convolution fusion | flops 17965056 | bytes 1143876 | tf_op jit(solution)/shard_map/dot_general | solution.py:155
  3.5 0.1 select_reduce_fusion
  3.6 0.1 dynamic_slice.7
  3.7 1.1 fusion.6
  4.8 0.1 fusion.49
  4.9 0.1 multiply_cosine_fusion.1
  5.0 0.1 subtract_convert_fusion
  5.1 0.1 pad_maximum_fusion
  5.3 30.2 %all-gather = bf16[16,17,256]{2,1,0:T(8,128)(2,1)S(1)} all-gather(bf16[1,17,256]{2,1,0:T(8,128)(2,1)S(1)} %reshape.327), channel_id=1, replica_groups=mesh['seq_hi'=4,'seq_lo'=16,'tp'=8] {'seq_lo'}, dimensions={0}, use_global_device_ids=true | all-gather | bytes 147968 | tf_op jit(solution)/shard_map/all_gather | solution.py:179
  35.4 0.1 reshape.328
  35.5 11.4 %all_gather.7.q_ref = bf16[1088,256]{1,0:T(8,128)(2,1)} all-gather(bf16[272,256]{1,0:T(8,128)(2,1)S(1)} %reshape.328), channel_id=1, replica_groups=mesh['seq_hi'=4,'seq_lo'=16,'tp'=8] {'seq_hi'}, dimensions={0}, use_global_device_ids=true | all-gather | bytes 696320 | tf_op jit(solution)/shard_map/all_gather | solution.py:178
  46.9 0.2 convolution_bitcast_fusion
  47.1 0.1 fusion.41
  47.3 0.6 pad_bitcast_fusion.np_ref
  47.9 0.5 pad_bitcast_fusion.1.nr_ref
  48.4 0.2 convolution_convert_fusion.1
  49.3 0.1 copy.25
  49.4 0.1 reduce-window.8
  49.5 0.1 reduce.2
  49.6 0.8 fusion.8
  50.4 0.6 add_subtract_fusion.kp_ref
  51.0 0.7 fusion.20.nk_ref
  51.7 0.6 concatenate.35.nv_ref
  52.3 12.8 %shard_map.100 = (bf16[1088,256]{1,0:T(8,128)(2,1)}, f32[1088,2]{1,0:T(8,128)}) custom-call(bf16[1088,256]{1,0:T(8,128)(2,1)} %all_gather.7.q_ref, s32[1088,1]{1,0:T(8,128)} %get-tuple-element.26.qr_ref, s32[1088,1]{1,0:T(8,128)} %get-tuple-element.27.qp_ref, bf16[2048,128]{1,0:T(8,128)(2,1)} %k_ref.1, bf16[2048,128]{1,0:T(8,128)(2,1)} %v_ref.1, ...), custom_call_target="tpu_custom_call" | custom-call | tf_op jit(solution)/shard_map/pallas_call | solution.py:98
  65.1 1.3 fusion.12
  66.4 0.2 reshape.318
  66.6 0.2 reshape.319
  66.8 0.2 reshape.320
  67.0 0.6 reshape.317
  67.6 0.3 concatenate.38
  67.9 0.5 broadcast.290
  68.4 1.0 reduce.3
  69.5 0.9 reshape.332
  70.4 9.2 %all-to-all-start = ((bf16[64,2,2304]{2,1,0:T(2,128)(2,1)}), bf16[64,2,2304]{2,1,0:T(2,128)(2,1)S(1)}, u32[]{:S(2)}, u32[]{:S(2)}) async-start(bf16[64,2,2304]{2,1,0:T(2,128)(2,1)} %reshape.332), calls=%async_computation | async-start | bytes 1179648 | tf_op jit(solution)/shard_map/all_to_all | solution.py:200
  79.6 21.5 %all-to-all-done = bf16[64,2,2304]{2,1,0:T(2,128)(2,1)S(1)} async-done(((bf16[64,2,2304]{2,1,0:T(2,128)(2,1)}), bf16[64,2,2304]{2,1,0:T(2,128)(2,1)S(1)}, u32[]{:S(2)}, u32[]{:S(2)}) %all-to-all-start) | async-done | bytes 589856 | tf_op jit(solution)/shard_map/all_to_all | solution.py:200
  101.1 0.5 reshape.333
  101.6 0.1 copy.34
  101.7 0.1 copy.27
  101.8 0.1 fusion.47
  101.9 0.2 fusion.26
  102.1 0.1 div.52
  102.2 0.1 div.53
  102.3 0.8 fusion.4
  103.1 0.2 convolution_convert_fusion
  103.4 22.6 %all_to_all.17 = bf16[8,17,256]{2,1,0:T(8,128)(2,1)S(1)} all-to-all(bf16[8,17,256]{2,1,0:T(8,128)(2,1)S(1)} %bitcast.44), channel_id=1, replica_groups=mesh['seq_hi'=4,'seq_lo'=16,'tp'=8] {'tp'}, dimensions={0} | all-to-all | bytes 139264 | tf_op jit(solution)/shard_map/all_to_all | solution.py:219
  126.0 0.6 reduce_sum.78
  (30 shorter events, 0.2 us)
Async XLA Ops:
  0.0 103.1 %copy-start = (bf16[256,2048]{1,0:T(8,128)(2,1)S(1)}, bf16[256,2048]{1,0:T(8,128)(2,1)}, u32[]{:S(2)}) copy-start(bf16[256,2048]{1,0:T(8,128)(2,1)} %param.15) | copy-start | bytes 3145732
  0.0 3.5 %copy-start.5 = (s32[66]{0:T(128)S(1)}, s32[66]{0:T(128)}, u32[]{:S(2)}) copy-start(s32[66]{0:T(128)} %param.18) | copy-start | bytes 796
  3.7 43.2 %copy-start.1 = (bf16[17,2048]{1,0:T(8,128)(2,1)S(1)}, bf16[17,2048]{1,0:T(8,128)(2,1)}, u32[]{:S(2)}) copy-start(bf16[17,2048]{1,0:T(8,128)(2,1)} %param.10) | copy-start | bytes 208900
  3.7 43.2 %copy-start.3 = (bf16[2048,128]{1,0:T(8,128)(2,1)S(1)}, bf16[2048,128]{1,0:T(8,128)(2,1)}, u32[]{:S(2)}) copy-start(bf16[2048,128]{1,0:T(8,128)(2,1)} %param.13) | copy-start | bytes 1572868
  4.8 43.6 %copy-start.4 = (bf16[2048,128]{1,0:T(8,128)(2,1)S(1)}, bf16[2048,128]{1,0:T(8,128)(2,1)}, u32[]{:S(2)}) copy-start(bf16[2048,128]{1,0:T(8,128)(2,1)} %param.14) | copy-start | bytes 1572868
  65.1 1.8 %copy-start.2 = (bf16[1088,256]{1,0:T(8,128)(2,1)S(1)}, bf16[1088,256]{1,0:T(8,128)(2,1)}, u32[]{:S(2)}) copy-start(bf16[1088,256]{1,0:T(8,128)(2,1)} %get-tuple-element.7) | copy-start | bytes 1671172
  70.4 30.7 %all-to-all-start = ((bf16[64,2,2304]{2,1,0:T(2,128)(2,1)}), bf16[64,2,2304]{2,1,0:T(2,128)(2,1)S(1)}, u32[]{:S(2)}, u32[]{:S(2)}) async-start(bf16[64,2,2304]{2,1,0:T(2,128)(2,1)} %reshape.332), calls=%async_computation | async-start | bytes 1179648 | tf_op jit(solution)/shard_map/all_to_all | solution.py:200

commit v10 on v9

--- a/solution.py
+++ b/solution.py
@@ -87,7 +87,7 @@
     lw_ref[...] = jnp.concatenate(tops, axis=1)
 
 
-def attend(q, q_req, q_pos, keys, values, k_req, k_pos, new_k, new_v, n_req, n_pos, block_rows=544):
+def attend(q, q_req, q_pos, keys, values, k_req, k_pos, new_k, new_v, n_req, n_pos, block_rows=1088):
     rows, width = q.shape
     heads = width // HD
     slots = keys.shape[0]

time: 127 us -> 127 us (level)
  no operation moved by 1% of the time
where the time goes in v10:
time: 127 us
  blocking collectives  64.2 us (51%)
  waiting for transfers between devices  21.5 us (17%)
  Pallas kernels  12.7 us (10%)
  starting transfers between devices  9.15 us (7%)
  other arithmetic  9.14 us (7%)
  local copies, waits for them, and re-layouts  6.02 us (5%)
  matrix products  3.07 us (2%)
    all_gather x1, blocking collectives, per_device(): lax.all_gather(queries, SEQ[1], axis=0, tiled=True)  30.2 us
    all_to_all x1, blocking collectives, per_device(): blocks = lax.all_to_all(blocks, 'tp', 0, 0, tiled=True)  22.6 us
    all_to_all x1, waiting for transfers between devices, per_device(): received = lax.all_to_all(packed, SEQ, 0, 0, tiled=True)  21.5 us
    pallas_call x1, Pallas kernels, attend(): pl.pallas_call(functools.partial(attend_kernel, heads=heads), grid=grid,...  12.7 us
    all_gather x1, blocking collectives, per_device(): lax.all_gather(lax.all_gather(queries, SEQ[1], axis=0, tiled=True), SEQ[0...  11.4 us
    all_to_all x1, starting transfers between devices, per_device(): received = lax.all_to_all(packed, SEQ, 0, 0, tiled=True)  9.15 us
  transfers between devices with their start and end apart: 1, of which 1 were waited for; matrix products, arithmetic and copies ran while one was open for 0% of the time, Pallas kernels for 0%

profile of v10, /device:TPU:1, one launch (start us, length us, event | category | flops | bytes accessed | tf_op | source)
XLA Modules:
  0.0 126.7 jit_solution(3711357626125763685)
XLA Ops:
  0.1 0.8 convert_element_type.52
  0.8 1.0 fusion.15
  1.9 1.6 %fusion.45 = f32[17,256]{1,0:T(8,128)S(1)} fusion(bf16[2048,256]{1,0:T(8,128)(2,1)} %param.12, bf16[17,2048]{1,0:T(8,128)(2,1)} %param.10, f32[2048]{0:T(1024)S(1)} %convert_element_type.52, f32[17]{0:T(128)S(1)} %add_rsqrt_fusion), kind=kOutput, calls=%fused_computation.97 | convolution fusion | flops 17965056 | bytes 1143876 | tf_op jit(solution)/shard_map/dot_general | solution.py:155
  3.5 0.1 select_reduce_fusion
  3.6 0.1 dynamic_slice.7
  3.7 1.1 fusion.6
  4.8 0.1 fusion.49
  4.9 0.1 multiply_cosine_fusion.1
  5.0 0.1 subtract_convert_fusion
  5.1 0.1 pad_maximum_fusion
  5.3 30.2 %all-gather = bf16[16,17,256]{2,1,0:T(8,128)(2,1)S(1)} all-gather(bf16[1,17,256]{2,1,0:T(8,128)(2,1)S(1)} %reshape.327), channel_id=1, replica_groups=mesh['seq_hi'=4,'seq_lo'=16,'tp'=8] {'seq_lo'}, dimensions={0}, use_global_device_ids=true | all-gather | bytes 147968 | tf_op jit(solution)/shard_map/all_gather | solution.py:179
  35.4 0.1 reshape.328
  35.5 11.4 %all_gather.7.q_ref = bf16[1088,256]{1,0:T(8,128)(2,1)} all-gather(bf16[272,256]{1,0:T(8,128)(2,1)S(1)} %reshape.328), channel_id=1, replica_groups=mesh['seq_hi'=4,'seq_lo'=16,'tp'=8] {'seq_hi'}, dimensions={0}, use_global_device_ids=true | all-gather | bytes 696320 | tf_op jit(solution)/shard_map/all_gather | solution.py:178
  46.9 0.2 convolution_bitcast_fusion
  47.1 0.1 fusion.41
  47.3 0.6 pad_bitcast_fusion.np_ref
  47.9 0.5 pad_bitcast_fusion.1.nr_ref
  48.4 0.2 convolution_convert_fusion.1
  49.3 0.1 copy.25
  49.4 0.1 reduce-window.8
  49.5 0.1 reduce.2
  49.6 0.8 fusion.8
  50.4 0.6 add_subtract_fusion.kp_ref
  51.0 0.7 fusion.20.nk_ref
  51.7 0.6 concatenate.35.nv_ref
  52.3 12.7 %shard_map.100 = (bf16[1088,256]{1,0:T(8,128)(2,1)}, f32[1088,2]{1,0:T(8,128)}) custom-call(bf16[1088,256]{1,0:T(8,128)(2,1)} %all_gather.7.q_ref, s32[1088,1]{1,0:T(8,128)} %get-tuple-element.26.qr_ref, s32[1088,1]{1,0:T(8,128)} %get-tuple-element.27.qp_ref, bf16[2048,128]{1,0:T(8,128)(2,1)} %k_ref.1, bf16[2048,128]{1,0:T(8,128)(2,1)} %v_ref.1, ...), custom_call_target="tpu_custom_call" | custom-call | tf_op jit(solution)/shard_map/pallas_call | solution.py:98
  65.0 1.3 fusion.12
  66.3 0.2 reshape.318
  66.5 0.2 reshape.319
  66.7 0.2 reshape.320
  66.9 0.8 reshape.317
  67.7 0.3 concatenate.38
  67.9 0.5 broadcast.290
  68.5 1.0 reduce.3
  69.5 0.9 reshape.332
  70.5 9.2 %all-to-all-start = ((bf16[64,2,2304]{2,1,0:T(2,128)(2,1)}), bf16[64,2,2304]{2,1,0:T(2,128)(2,1)S(1)}, u32[]{:S(2)}, u32[]{:S(2)}) async-start(bf16[64,2,2304]{2,1,0:T(2,128)(2,1)} %reshape.332), calls=%async_computation | async-start | bytes 1179648 | tf_op jit(solution)/shard_map/all_to_all | solution.py:200
  79.6 21.5 %all-to-all-done = bf16[64,2,2304]{2,1,0:T(2,128)(2,1)S(1)} async-done(((bf16[64,2,2304]{2,1,0:T(2,128)(2,1)}), bf16[64,2,2304]{2,1,0:T(2,128)(2,1)S(1)}, u32[]{:S(2)}, u32[]{:S(2)}) %all-to-all-start) | async-done | bytes 589856 | tf_op jit(solution)/shard_map/all_to_all | solution.py:200
  101.1 0.5 reshape.333
  101.6 0.1 copy.34
  101.7 0.1 copy.27
  101.8 0.1 fusion.47
  101.9 0.2 fusion.26
  102.1 0.1 div.52
  102.2 0.1 div.53
  102.3 0.8 fusion.4
  103.1 0.2 convolution_convert_fusion
  103.5 22.6 %all_to_all.17 = bf16[8,17,256]{2,1,0:T(8,128)(2,1)S(1)} all-to-all(bf16[8,17,256]{2,1,0:T(8,128)(2,1)S(1)} %bitcast.44), channel_id=1, replica_groups=mesh['seq_hi'=4,'seq_lo'=16,'tp'=8] {'tp'}, dimensions={0} | all-to-all | bytes 139264 | tf_op jit(solution)/shard_map/all_to_all | solution.py:219
  126.1 0.6 reduce_sum.78
  (30 shorter events, 0.2 us)
Async XLA Ops:
  0.0 103.1 %copy-start = (bf16[256,2048]{1,0:T(8,128)(2,1)S(1)}, bf16[256,2048]{1,0:T(8,128)(2,1)}, u32[]{:S(2)}) copy-start(bf16[256,2048]{1,0:T(8,128)(2,1)} %param.15) | copy-start | bytes 3145732
  0.0 3.5 %copy-start.5 = (s32[66]{0:T(128)S(1)}, s32[66]{0:T(128)}, u32[]{:S(2)}) copy-start(s32[66]{0:T(128)} %param.18) | copy-start | bytes 796
  3.7 43.2 %copy-start.1 = (bf16[17,2048]{1,0:T(8,128)(2,1)S(1)}, bf16[17,2048]{1,0:T(8,128)(2,1)}, u32[]{:S(2)}) copy-start(bf16[17,2048]{1,0:T(8,128)(2,1)} %param.10) | copy-start | bytes 208900
  3.7 43.2 %copy-start.3 = (bf16[2048,128]{1,0:T(8,128)(2,1)S(1)}, bf16[2048,128]{1,0:T(8,128)(2,1)}, u32[]{:S(2)}) copy-start(bf16[2048,128]{1,0:T(8,128)(2,1)} %param.13) | copy-start | bytes 1572868
  4.8 43.6 %copy-start.4 = (bf16[2048,128]{1,0:T(8,128)(2,1)S(1)}, bf16[2048,128]{1,0:T(8,128)(2,1)}, u32[]{:S(2)}) copy-start(bf16[2048,128]{1,0:T(8,128)(2,1)} %param.14) | copy-start | bytes 1572868
  65.0 1.8 %copy-start.2 = (bf16[1088,256]{1,0:T(8,128)(2,1)S(1)}, bf16[1088,256]{1,0:T(8,128)(2,1)}, u32[]{:S(2)}) copy-start(bf16[1088,256]{1,0:T(8,128)(2,1)} %get-tuple-element.7) | copy-start | bytes 1671172
  70.5 30.7 %all-to-all-start = ((bf16[64,2,2304]{2,1,0:T(2,128)(2,1)}), bf16[64,2,2304]{2,1,0:T(2,128)(2,1)S(1)}, u32[]{:S(2)}, u32[]{:S(2)}) async-start(bf16[64,2,2304]{2,1,0:T(2,128)(2,1)} %reshape.332), calls=%async_computation | async-start | bytes 1179648 | tf_op jit(solution)/shard_map/all_to_all | solution.py:200

commit v11 on v10

--- a/solution.py
+++ b/solution.py
@@ -53,7 +53,7 @@
 
 
 def attend_kernel(
-    q_ref, qr_ref, qp_ref, k_ref, v_ref, kr_ref, kp_ref, nk_ref, nv_ref, nr_ref, np_ref,
+    q_ref, qr_ref, qp_ref, k_ref, v_ref, kr_ref, nk_ref, nv_ref, nr_ref, np_ref,
     avg_ref, lw_ref, *, heads
 ):
     seen_cache = qr_ref[...] == kr_ref[...]
@@ -87,7 +87,7 @@
     lw_ref[...] = jnp.concatenate(tops, axis=1)
 
 
-def attend(q, q_req, q_pos, keys, values, k_req, k_pos, new_k, new_v, n_req, n_pos, block_rows=1088):
+def attend(q, q_req, q_pos, keys, values, k_req, new_k, new_v, n_req, n_pos, block_rows=544):
     rows, width = q.shape
     heads = width // HD
     slots = keys.shape[0]
@@ -105,7 +105,6 @@
             pl.BlockSpec((slots, HD), whole),
             pl.BlockSpec((slots, HD), whole),
             pl.BlockSpec((1, slots), whole),
-            pl.BlockSpec((1, slots), whole),
             pl.BlockSpec((fresh, HD), whole),
             pl.BlockSpec((fresh, HD), whole),
             pl.BlockSpec((1, fresh), whole),
@@ -121,7 +120,7 @@
         ],
     )(
         q, q_req.reshape(rows, 1), q_pos.reshape(rows, 1), keys, values,
-        k_req.reshape(1, slots), k_pos.reshape(1, slots),
+        k_req.reshape(1, slots),
         new_k, new_v, n_req.reshape(1, fresh), n_pos.reshape(1, fresh),
     )
 
@@ -174,12 +173,12 @@
     )
     new_req = jnp.concatenate([my_request, jnp.full((extra,), -1, jnp.int32)], axis=0)
     new_pos = jnp.concatenate([my_position, jnp.zeros((extra,), jnp.int32)], axis=0)
-    slot_request, slot_position = slot_layout(block_of_shard[0], cache_keys.shape[0], cached_len)
+    slot_request, _ = slot_layout(block_of_shard[0], cache_keys.shape[0], cached_len)
     gathered = lax.all_gather(
         lax.all_gather(queries, SEQ[1], axis=0, tiled=True), SEQ[0], axis=0, tiled=True
     )
     average, log_weight = attend(
-        gathered, request_all, position_all, cache_keys, cache_values, slot_request, slot_position,
+        gathered, request_all, position_all, cache_keys, cache_values, slot_request,
         new_k, new_v, new_req, new_pos,
     )
     pairs = tok_rows * q_heads

time: 127 us -> 126 us (level)
  no operation moved by 1% of the time
where the time goes in v11:
time: 126 us
  blocking collectives  64.2 us (51%)
  waiting for transfers between devices  21.5 us (17%)
  Pallas kernels  12.8 us (10%)
  starting transfers between devices  9.15 us (7%)
  other arithmetic  8.5 us (7%)
  local copies, waits for them, and re-layouts  5.74 us (5%)
  matrix products  3.07 us (2%)
    all_gather x1, blocking collectives, per_device(): lax.all_gather(queries, SEQ[1], axis=0, tiled=True)  30.2 us
    all_to_all x1, blocking collectives, per_device(): blocks = lax.all_to_all(blocks, 'tp', 0, 0, tiled=True)  22.6 us
    all_to_all x1, waiting for transfers between devices, per_device(): received = lax.all_to_all(packed, SEQ, 0, 0, tiled=True)  21.5 us
    pallas_call x1, Pallas kernels, attend(): pl.pallas_call(functools.partial(attend_kernel, heads=heads), grid=grid,...  12.8 us
    all_gather x1, blocking collectives, per_device(): lax.all_gather(lax.all_gather(queries, SEQ[1], axis=0, tiled=True), SEQ[0...  11.4 us
    all_to_all x1, starting transfers between devices, per_device(): received = lax.all_to_all(packed, SEQ, 0, 0, tiled=True)  9.15 us
  transfers between devices with their start and end apart: 1, of which 1 were waited for; matrix products, arithmetic and copies ran while one was open for 0% of the time, Pallas kernels for 0%

profile of v11, /device:TPU:1, one launch (start us, length us, event | category | flops | bytes accessed | tf_op | source)
XLA Modules:
  0.0 125.9 jit_solution(6449035651984706092)
XLA Ops:
  0.1 0.8 convert_element_type.52
  0.8 1.0 fusion.13
  1.9 1.6 %fusion.43 = f32[17,256]{1,0:T(8,128)S(1)} fusion(bf16[2048,256]{1,0:T(8,128)(2,1)} %param.12, bf16[17,2048]{1,0:T(8,128)(2,1)} %param.10, f32[2048]{0:T(1024)S(1)} %convert_element_type.52, f32[17]{0:T(128)S(1)} %add_rsqrt_fusion), kind=kOutput, calls=%fused_computation.93 | convolution fusion | flops 17965056 | bytes 1143876 | tf_op jit(solution)/shard_map/dot_general | solution.py:154
  3.5 0.1 select_reduce_fusion
  3.6 0.1 dynamic_slice.7
  3.7 1.1 fusion.6
  4.8 0.1 fusion.47
  4.9 0.1 multiply_cosine_fusion.1
  5.0 0.1 subtract_convert_fusion
  5.1 0.1 pad_maximum_fusion
  5.3 30.2 %all-gather = bf16[16,17,256]{2,1,0:T(8,128)(2,1)S(1)} all-gather(bf16[1,17,256]{2,1,0:T(8,128)(2,1)S(1)} %reshape.312), channel_id=1, replica_groups=mesh['seq_hi'=4,'seq_lo'=16,'tp'=8] {'seq_lo'}, dimensions={0}, use_global_device_ids=true | all-gather | bytes 147968 | tf_op jit(solution)/shard_map/all_gather | solution.py:178
  35.4 0.1 reshape.313
  35.5 11.4 %all_gather.7.q_ref = bf16[1088,256]{1,0:T(8,128)(2,1)} all-gather(bf16[272,256]{1,0:T(8,128)(2,1)S(1)} %reshape.313), channel_id=1, replica_groups=mesh['seq_hi'=4,'seq_lo'=16,'tp'=8] {'seq_hi'}, dimensions={0}, use_global_device_ids=true | all-gather | bytes 696320 | tf_op jit(solution)/shard_map/all_gather | solution.py:177
  46.9 0.0 copy-done.1
  46.9 0.2 convolution_bitcast_fusion
  47.1 0.1 fusion.39
  47.3 0.5 pad_bitcast_fusion.np_ref
  47.8 0.5 pad_bitcast_fusion.1.nr_ref
  48.3 0.2 convolution_convert_fusion.1
  48.5 0.1 copy.25
  48.7 0.1 reduce-window.8
  48.8 0.1 reduce.2
  49.5 0.7 fusion.18.nk_ref
  50.2 0.6 concatenate.35.nv_ref
  50.9 0.7 convert_reduce_fusion
  51.6 12.8 %shard_map.100 = (bf16[1088,256]{1,0:T(8,128)(2,1)}, f32[1088,2]{1,0:T(8,128)}) custom-call(bf16[1088,256]{1,0:T(8,128)(2,1)} %all_gather.7.q_ref, s32[1088,1]{1,0:T(8,128)} %get-tuple-element.24.qr_ref, s32[1088,1]{1,0:T(8,128)} %get-tuple-element.25.qp_ref, bf16[2048,128]{1,0:T(8,128)(2,1)} %k_ref.1, bf16[2048,128]{1,0:T(8,128)(2,1)} %v_ref.1, ...), custom_call_target="tpu_custom_call" | custom-call | tf_op jit(solution)/shard_map/pallas_call | solution.py:98
  64.4 1.3 %fusion.10 = (bf16[1088,2]{1,0:T(8,128)(2,1)S(1)}, bf16[1088,2]{1,0:T(8,128)(2,1)S(1)}, bf16[1088,2]{1,0:T(8,128)(2,1)S(1)}) fusion(f32[1088,2]{1,0:T(8,128)} %get-tuple-element.8), kind=kLoop, calls=%fused_computation.27 | loop fusion | flops 15232 | bytes 21760 | tf_op jit(solution)/shard_map/convert_element_type | solution.py:194
  65.6 0.2 reshape.303
  65.8 0.2 reshape.304
  66.0 0.2 reshape.305
  66.2 0.6 reshape.302
  66.8 0.3 concatenate.38
  67.1 0.5 broadcast.283
  67.6 1.0 reduce.3
  68.7 0.9 reshape.317
  69.6 9.1 %all-to-all-start = ((bf16[64,2,2304]{2,1,0:T(2,128)(2,1)}), bf16[64,2,2304]{2,1,0:T(2,128)(2,1)S(1)}, u32[]{:S(2)}, u32[]{:S(2)}) async-start(bf16[64,2,2304]{2,1,0:T(2,128)(2,1)} %reshape.317), calls=%async_computation | async-start | bytes 1179648 | tf_op jit(solution)/shard_map/all_to_all | solution.py:199
  78.8 21.5 %all-to-all-done = bf16[64,2,2304]{2,1,0:T(2,128)(2,1)S(1)} async-done(((bf16[64,2,2304]{2,1,0:T(2,128)(2,1)}), bf16[64,2,2304]{2,1,0:T(2,128)(2,1)S(1)}, u32[]{:S(2)}, u32[]{:S(2)}) %all-to-all-start) | async-done | bytes 589856 | tf_op jit(solution)/shard_map/all_to_all | solution.py:199
  100.3 0.5 reshape.318
  100.8 0.1 copy.34
  100.9 0.1 copy.27
  101.0 0.1 fusion.45
  101.1 0.2 fusion.24
  101.3 0.1 div.52
  101.4 0.1 div.53
  101.5 0.8 fusion.4
  102.3 0.2 convolution_convert_fusion
  102.6 22.6 %all_to_all.17 = bf16[8,17,256]{2,1,0:T(8,128)(2,1)S(1)} all-to-all(bf16[8,17,256]{2,1,0:T(8,128)(2,1)S(1)} %bitcast.43), channel_id=1, replica_groups=mesh['seq_hi'=4,'seq_lo'=16,'tp'=8] {'tp'}, dimensions={0} | all-to-all | bytes 139264 | tf_op jit(solution)/shard_map/all_to_all | solution.py:218
  125.3 0.6 reduce_sum.65
  (29 shorter events, 0.2 us)
Async XLA Ops:
  0.0 102.3 %copy-start = (bf16[256,2048]{1,0:T(8,128)(2,1)S(1)}, bf16[256,2048]{1,0:T(8,128)(2,1)}, u32[]{:S(2)}) copy-start(bf16[256,2048]{1,0:T(8,128)(2,1)} %param.15) | copy-start | bytes 3145732
  0.0 3.5 %copy-start.5 = (s32[66]{0:T(128)S(1)}, s32[66]{0:T(128)}, u32[]{:S(2)}) copy-start(s32[66]{0:T(128)} %param.18) | copy-start | bytes 796
  3.7 43.2 %copy-start.1 = (bf16[17,2048]{1,0:T(8,128)(2,1)S(1)}, bf16[17,2048]{1,0:T(8,128)(2,1)}, u32[]{:S(2)}) copy-start(bf16[17,2048]{1,0:T(8,128)(2,1)} %param.10) | copy-start | bytes 208900
  3.7 43.2 %copy-start.3 = (bf16[2048,128]{1,0:T(8,128)(2,1)S(1)}, bf16[2048,128]{1,0:T(8,128)(2,1)}, u32[]{:S(2)}) copy-start(bf16[2048,128]{1,0:T(8,128)(2,1)} %param.13) | copy-start | bytes 1572868
  4.8 43.5 %copy-start.4 = (bf16[2048,128]{1,0:T(8,128)(2,1)S(1)}, bf16[2048,128]{1,0:T(8,128)(2,1)}, u32[]{:S(2)}) copy-start(bf16[2048,128]{1,0:T(8,128)(2,1)} %param.14) | copy-start | bytes 1572868
  64.4 1.8 %copy-start.2 = (bf16[1088,256]{1,0:T(8,128)(2,1)S(1)}, bf16[1088,256]{1,0:T(8,128)(2,1)}, u32[]{:S(2)}) copy-start(bf16[1088,256]{1,0:T(8,128)(2,1)} %get-tuple-element.7) | copy-start | bytes 1671172
  69.6 30.7 %all-to-all-start = ((bf16[64,2,2304]{2,1,0:T(2,128)(2,1)}), bf16[64,2,2304]{2,1,0:T(2,128)(2,1)S(1)}, u32[]{:S(2)}, u32[]{:S(2)}) async-start(bf16[64,2,2304]{2,1,0:T(2,128)(2,1)} %reshape.317), calls=%async_computation | async-start | bytes 1179648 | tf_op jit(solution)/shard_map/all_to_all | solution.py:199
